TPU v7x, 32 devices: a whole 2x2x4 slice. The times are simulated.
32 devices in a mesh: section: 4 (over y, x), ctx: 8 (over z, core).
Axes of the slice: x: 2, y: 2, z: 4, core: 2. Of those that a mesh axis runs over, the one named last changes fastest.
Arguments:
- queries: bfloat16 [4, 1024, 2048], P('section', 'ctx'), may hold values from -4.5 to 4.5
- keys_values: bfloat16 [4, 1024, 1024], P('section', 'ctx'), may hold values from -4.5 to 4.5
- mix_in: bfloat16 [4, 3, 1024, 4096], P('section', None, 'ctx'), may hold values from -11.5 to 4.5
- proj_bc: bfloat16 [4, 1024, 16], P('section', 'ctx'), may hold values from -12 to 12
- attn_cot: bfloat16 [4, 1024, 2048], P('section', 'ctx'), may hold values from -6 to 6
- mamba_cot: bfloat16 [4, 1024, 4096], P('section', 'ctx'), may hold values from -6 to 6
- conv_weight: float32 [4, 4, 4096], P('section'), may hold values from -3 to 3
- conv_bias: float32 [4, 4096], P('section'), may hold values from -3 to 3
- a_log: float32 [4, 8, 4096], P('section'), may hold values from -0.7 to 0.7
- skip_gain: float32 [4, 4096], P('section'), may hold values from 0.5 to 4
Outputs:
- attn_out: bfloat16 [4, 1024, 2048], P('section', 'ctx')
- mamba_out: bfloat16 [4, 1024, 4096], P('section', 'ctx')
- query_grads: bfloat16 [4, 1024, 2048], P('section', 'ctx')
- pair_grads: bfloat16 [4, 1024, 1024], P('section', 'ctx')
- mix_grads: bfloat16 [4, 3, 1024, 4096], P('section', None, 'ctx')
- bc_grads: bfloat16 [4, 1024, 16], P('section', 'ctx')
- conv_weight_grad: float32 [4, 4, 4096], P('section')
- conv_bias_grad: float32 [4, 4096], P('section')
- a_log_grad: float32 [4, 8, 4096], P('section')
- skip_grad: float32 [4, 4096], P('section')
All inputs are finite; a program needn't handle non-finite values.
Results may differ from a plain program's by a relative error of at most 0.019.
Values may be sent and summed in bfloat16 or wider, within the bound.
No kernel may reach another device: no remote copies, remote signals or barrier semaphores. Data moves between devices by JAX's collectives and lax.ppermute only.
A program may use at most 256 MiB of HBM per device.

v0:
```python
from functools import partial

import jax
import jax.numpy as jnp
from jax import lax
from jax.sharding import PartitionSpec as P

C = 4096
NSTATE = 8
KCONV = 4
HEADS = 16
KVHEADS = 4
HDIM = 128


def shifted(block, axis, distance):
    devices = range(lax.axis_size(axis))
    route = [((i - distance) % len(devices), i) for i in devices]
    return lax.ppermute(block, axis, route)


def passed_along(shard, axis, by):
    devices = lax.axis_size(axis)
    pairs = [(i, i + by) for i in range(devices) if 0 <= i + by < devices]
    return lax.ppermute(shard, axis, pairs)


def carried_in(shard, axis, join, neutral, backward):
    count = lax.axis_size(axis)
    place = lax.axis_index(axis)
    ahead = count - 1 - place if backward else place
    gathered = jax.tree.map(
        lambda a, kind: lax.all_gather(a.astype(kind), axis), shard, (jnp.bfloat16, jnp.bfloat16)
    )
    state = jax.tree.map(lambda a, e: jnp.zeros_like(a) + jnp.asarray(e, a.dtype), shard, neutral)

    def one(hop, state):
        source = count - 1 - hop if backward else hop
        return join(
            state,
            jax.tree.map(
                lambda a, own: lax.dynamic_index_in_dim(a, source, 0, False).astype(own.dtype),
                gathered,
                shard,
            ),
        )

    return lax.fori_loop(0, ahead, one, state)


def shortened(shard):

    def short(part):
        return part.astype(jnp.bfloat16) if part.dtype == jnp.float32 else part

    return jax.tree.map(short, shard)


def combine_pairs(earlier, later):
    return (earlier[0] * later[0], later[0] * earlier[1] + later[1])


def silu_slope(value):
    sigmoid_v = jax.nn.sigmoid(value)
    return sigmoid_v * (1.0 + value * (1.0 - sigmoid_v))


def to_blocks(matrix, block_width):
    return matrix.reshape(matrix.shape[0], matrix.shape[1] // block_width, block_width).transpose(
        1, 0, 2
    )


def from_blocks(stacked):
    return stacked.transpose(1, 0, 2).reshape(stacked.shape[1], stacked.shape[0] * stacked.shape[2])


def attention_group(group_index, query_heads, grad_heads, key_whole, first_row, softmax_scale):
    query_g = lax.dynamic_index_in_dim(query_heads, group_index, 1, False)
    grad_g = lax.dynamic_index_in_dim(grad_heads, group_index, 1, False)
    pair_rows = lax.dynamic_index_in_dim(key_whole, group_index, 2, False)
    key_rows = pair_rows[:, 0]
    value_rows = pair_rows[:, 1]
    scores = (
        jnp.einsum("trd,sd->trs", query_g, key_rows, preferred_element_type=jnp.float32)
        * softmax_scale
    )
    query_pos = first_row + jnp.arange(query_g.shape[0], dtype=jnp.int32)
    key_pos = jnp.arange(key_rows.shape[0], dtype=jnp.int32)
    allowed = (key_pos[None, :] <= query_pos[:, None])[:, None, :]
    row_peak = jnp.max(jnp.where(allowed, scores, -jnp.inf), axis=-1, keepdims=True)
    row_total = jnp.sum(jnp.where(allowed, jnp.exp(scores - row_peak), 0.0), axis=-1, keepdims=True)
    probs_b = jnp.where(allowed, jnp.exp(scores - (row_peak + jnp.log(row_total))), 0.0).astype(
        jnp.bfloat16
    )
    output = jnp.einsum(
        "trs,sd->trd", probs_b, value_rows, preferred_element_type=jnp.float32
    ).astype(jnp.bfloat16)
    prob_slope = jnp.einsum("trd,sd->trs", grad_g, value_rows, preferred_element_type=jnp.float32)
    row_delta = jnp.sum(
        grad_g.astype(jnp.float32) * output.astype(jnp.float32), axis=-1, keepdims=True
    )
    score_grad = (probs_b.astype(jnp.float32) * (prob_slope - row_delta)).astype(jnp.bfloat16)
    query_grad = (
        jnp.einsum("trs,sd->trd", score_grad, key_rows, preferred_element_type=jnp.float32)
        * softmax_scale
    ).astype(jnp.bfloat16)
    return (output, query_grad, probs_b, score_grad)


def key_terms(probs_all, score_all, query_heads, grad_heads, softmax_scale):
    key_grad = (
        jnp.einsum("gtrs,tgrd->sgd", score_all, query_heads, preferred_element_type=jnp.float32)
        * softmax_scale
    )
    value_grad = jnp.einsum(
        "gtrs,tgrd->sgd", probs_all, grad_heads, preferred_element_type=jnp.float32
    )
    return jnp.stack([key_grad, value_grad], axis=1)


def end_states(pieces_in, b_proj, c_proj):
    step_k, moved_k, drive_k, rate_k = pieces_in
    cumulative = lax.cumsum(step_k, axis=0)
    whole_sum = cumulative[-1]
    ahead = jnp.exp((whole_sum[None, :] - cumulative)[:, None, :] * rate_k[None])
    state_end = jnp.sum(ahead * b_proj[:, :, None] * moved_k[:, None, :], axis=0)
    behind = jnp.exp(cumulative[:, None, :] * rate_k[None])
    adjoint_end = jnp.sum(behind * c_proj[:, :, None] * drive_k[:, None, :], axis=0)
    return (jnp.exp(whole_sum[None, :] * rate_k), state_end, adjoint_end)


def full_pass(pieces_in, b_proj, c_proj, sub_length):
    step_k, moved_k, drive_k, rate_k, inner_k, skip_k, start_state, start_adjoint = pieces_in
    row_count = step_k.shape[0]
    block_width = step_k.shape[1]
    splits = row_count // sub_length

    def in_subs(matrix):
        return matrix.reshape(splits, sub_length, matrix.shape[1])

    def forward_sub(running, pieces_sub):
        step_p, moved_p, b_part, c_part, drive_p = pieces_sub
        log_decay = lax.cumsum(step_p, axis=0)[:, None, :] * rate_k[None]
        inflow = b_part[:, :, None] * moved_p[:, None, :]
        states = jnp.exp(log_decay) * (
            running[None] + lax.cumsum(jnp.exp(-log_decay) * inflow, axis=0)
        )
        mixed_part = jnp.sum(states * c_part[:, :, None], axis=1)
        c_part_grad = jnp.sum(states * drive_p[:, None, :], axis=2)
        return (states[-1], (states, running, mixed_part, c_part_grad))

    _, (states, priors, mixed_parts, c_grads) = lax.scan(
        forward_sub,
        start_state,
        (in_subs(step_k), in_subs(moved_k), in_subs(b_proj), in_subs(c_proj), in_subs(drive_k)),
    )

    def backward_sub(carry, pieces_sub):
        running, rate_total = carry
        step_p, drive_p, c_part, b_part, moved_p, states_p, prior_p = pieces_sub
        log_decay = lax.cumsum(step_p, axis=0)[:, None, :] * rate_k[None]
        source = c_part[:, :, None] * drive_p[:, None, :]
        tail_sum = (
            lax.cumsum(jnp.exp(log_decay) * source, axis=0, reverse=True)
            + jnp.exp(log_decay[-1])[None] * running
        )
        adjoints = jnp.exp(-log_decay) * tail_sum
        before = jnp.concatenate([prior_p[None], states_p[:-1]], axis=0)
        through = adjoints * before * jnp.exp(step_p[:, None, :] * rate_k[None])
        adjoint_b = jnp.sum(adjoints * b_part[:, :, None], axis=1)
        b_part_grad = jnp.sum(adjoints * moved_p[:, None, :], axis=2)
        through_rate = jnp.sum(through * rate_k[None], axis=1)
        rate_total = rate_total + jnp.sum(through * step_p[:, None, :], axis=0)
        return ((tail_sum[0], rate_total), (adjoint_b, b_part_grad, through_rate))

    start_carry = (start_adjoint, jnp.zeros_like(start_adjoint))
    (_, rate_grad), (adjoint_parts, b_grads, through_parts) = lax.scan(
        backward_sub,
        start_carry,
        (
            in_subs(step_k),
            in_subs(drive_k),
            in_subs(c_proj),
            in_subs(b_proj),
            in_subs(moved_k),
            states,
            priors,
        ),
        reverse=True,
    )
    adjoint_b = adjoint_parts.reshape(row_count, block_width)
    mixed_out = mixed_parts.reshape(row_count, block_width) + skip_k * inner_k
    step_grad = through_parts.reshape(row_count, block_width) + adjoint_b * inner_k
    inner_grad = adjoint_b * step_k + skip_k * drive_k
    b_grad = b_grads.reshape(row_count, -1)
    c_grad = c_grads.reshape(row_count, -1)
    skip_grad = jnp.sum(drive_k * inner_k, axis=0)
    return (mixed_out, step_grad, inner_grad, rate_grad, b_grad, c_grad, skip_grad)


def body(
    queries,
    keys_values,
    mix_in,
    proj_bc,
    attn_cot,
    mamba_cot,
    conv_weight,
    conv_bias,
    a_log,
    skip_gain,
):
    query_in, pair_in, mixture, proj_in = shifted(
        (queries[0], keys_values[0], mix_in[0], proj_bc[0]), "section", 1
    )
    attn_grad, mamba_grad = shifted((attn_cot[0], mamba_cot[0]), "section", -1)
    row_count = query_in.shape[0]
    group_size = HEADS // KVHEADS
    softmax_scale = HDIM ** (-0.5)
    first_row = lax.axis_index("ctx") * row_count
    pairs_whole = lax.all_gather(pair_in, "ctx", axis=0, tiled=True)
    seq_length = pairs_whole.shape[0]
    key_whole = pairs_whole.reshape(seq_length, 2, KVHEADS, HDIM)
    query_heads = query_in.reshape(row_count, KVHEADS, group_size, HDIM)
    grad_heads = attn_grad.reshape(row_count, KVHEADS, group_size, HDIM)

    def per_group(group_index):
        return attention_group(
            group_index, query_heads, grad_heads, key_whole, first_row, softmax_scale
        )

    outputs, query_grads, probs_all, score_all = lax.map(
        per_group, jnp.arange(KVHEADS, dtype=jnp.int32)
    )
    attn_out = outputs.transpose(1, 0, 2, 3).reshape(row_count, HEADS * HDIM)
    query_out = query_grads.transpose(1, 0, 2, 3).reshape(row_count, HEADS * HDIM)
    whole_term = key_terms(probs_all, score_all, query_heads, grad_heads, softmax_scale)
    key_sum = lax.psum_scatter(
        whole_term.astype(jnp.bfloat16), "ctx", scatter_dimension=0, tiled=True
    )
    pair_out = key_sum.reshape(row_count, 2 * KVHEADS * HDIM)
    signal = mixture[0]
    gating = mixture[1]
    unscaled_step = mixture[2]
    conv_rows = KCONV - 1
    rim_rows = passed_along(signal[row_count - conv_rows :], "ctx", 1)
    padded = jnp.concatenate([rim_rows, signal], axis=0).astype(jnp.float32)
    conv_taps = conv_weight[0]
    preact = conv_bias[0]
    for offset in range(KCONV):
        preact = preact + conv_taps[offset] * padded[offset : offset + row_count]
    inner_act = jax.nn.silu(preact)
    step_size = jax.nn.softplus(unscaled_step.astype(jnp.float32))
    decay_rate = -jnp.exp(a_log[0])
    b_proj = proj_in[:, :NSTATE].astype(jnp.float32)
    c_proj = proj_in[:, NSTATE:].astype(jnp.float32)
    gating_f = gating.astype(jnp.float32)
    gate_act = jax.nn.silu(gating_f)
    out_grad = mamba_grad.astype(jnp.float32)
    out_drive = out_grad * gate_act
    moved_in = step_size * inner_act
    block_width = min(C, 512)
    block_count = C // block_width
    sub_length = min(row_count, 32)
    step_blocks = to_blocks(step_size, block_width)
    moved_blocks = to_blocks(moved_in, block_width)
    drive_blocks = to_blocks(out_drive, block_width)
    rate_blocks = to_blocks(decay_rate, block_width)
    decays, state_ends, adjoint_ends = lax.map(
        partial(end_states, b_proj=b_proj, c_proj=c_proj),
        (step_blocks, moved_blocks, drive_blocks, rate_blocks),
    )
    unit_decays = jnp.ones_like(decays)
    zero_states = jnp.zeros_like(decays)
    _, state_in = carried_in(
        (decays, state_ends), "ctx", combine_pairs, (unit_decays, zero_states), False
    )
    _, adjoint_in = carried_in(
        (decays, adjoint_ends), "ctx", combine_pairs, (unit_decays, zero_states), True
    )
    results = lax.map(
        partial(full_pass, b_proj=b_proj, c_proj=c_proj, sub_length=sub_length),
        (
            step_blocks,
            moved_blocks,
            drive_blocks,
            rate_blocks,
            to_blocks(inner_act, block_width),
            skip_gain[0].reshape(block_count, block_width),
            state_in,
            adjoint_in,
        ),
    )
    mixed_out = from_blocks(results[0])
    step_grad = from_blocks(results[1])
    inner_grad = from_blocks(results[2])
    rate_grad = from_blocks(results[3])
    b_grad = jnp.sum(results[4], axis=0)
    c_grad = jnp.sum(results[5], axis=0)
    skip_grad = results[6].reshape(C)
    mamba_out = (mixed_out * gate_act).astype(jnp.bfloat16)
    gating_grad = out_grad * mixed_out * silu_slope(gating_f)
    raw_grad = step_grad * jax.nn.sigmoid(unscaled_step.astype(jnp.float32))
    pre_grad = inner_grad * silu_slope(preact)
    rim_after = passed_along(shortened(pre_grad[:conv_rows]), "ctx", -1)
    extended = jnp.concatenate([pre_grad, rim_after], axis=0)
    signal_grad = jnp.zeros_like(pre_grad)
    for offset in range(KCONV):
        signal_grad = (
            signal_grad
            + conv_taps[offset] * extended[conv_rows - offset : conv_rows - offset + row_count]
        )
    tap_grad = jnp.stack(
        [jnp.sum(pre_grad * padded[offset : offset + row_count], axis=0) for offset in range(KCONV)]
    )
    bias_grad = jnp.sum(pre_grad, axis=0)
    log_grad = rate_grad * decay_rate
    tap_sum, bias_sum, log_sum, skip_sum = (
        lax.psum(tap_grad.astype(jnp.bfloat16), "ctx").astype(jnp.float32),
        lax.psum(bias_grad.astype(jnp.bfloat16), "ctx").astype(jnp.float32),
        lax.psum(log_grad.astype(jnp.bfloat16), "ctx").astype(jnp.float32),
        lax.psum(skip_grad.astype(jnp.bfloat16), "ctx").astype(jnp.float32),
    )
    mix_out = jnp.stack([signal_grad, gating_grad, raw_grad]).astype(jnp.bfloat16)
    proj_out = jnp.concatenate([b_grad, c_grad], axis=1).astype(jnp.bfloat16)
    return (
        attn_out[None],
        mamba_out[None],
        query_out[None],
        pair_out[None],
        mix_out[None],
        proj_out[None],
        tap_sum[None],
        bias_sum[None],
        log_sum[None],
        skip_sum[None],
    )


def solution(mesh):
    placed = (
        P("section", "ctx", None),
        P("section", "ctx", None),
        P("section", None, "ctx", None),
        P("section", "ctx", None),
        P("section", "ctx", None),
        P("section", "ctx", None),
        P("section", None, None),
        P("section", None),
        P("section", None, None),
        P("section", None),
    )
    return jax.shard_map(
        body,
        mesh=mesh,
        in_specs=placed,
        out_specs=(
            P("section", "ctx", None),
            P("section", "ctx", None),
            P("section", "ctx", None),
            P("section", "ctx", None),
            P("section", None, "ctx", None),
            P("section", "ctx", None),
            P("section", None, None),
            P("section", None),
            P("section", None, None),
            P("section", None),
        ),
        check_vma=False,
    )
```

profile of v0, /device:TPU:0, one launch (start us, length us, event | category | flops | bytes accessed | tf_op | source)
XLA Modules:
  0.0 788.2 jit_solution(9875193067019897092)
XLA Ops:
  26.1 77.4 %collective-permute-done.4 = bf16[128,16]{1,0:T(8,128)(2,1)S(1)} collective-permute-done((bf16[128,16]{1,0:T(8,128)(2,1)S(1)}, bf16[128,16]{1,0:T(8,128)(2,1)S(1)}, u32[]{:S(2)}, u32[]{:S(2)}) %collective-permute-start.4) | collective-permute-done | bytes 4128 | tf_op jit(solution)/shard_map/ppermute | solution.py:19
  106.2 14.2 %collective-permute-done.1 = bf16[128,1024]{0,1:T(8,128)(2,1)S(1)} collective-permute-done((bf16[128,1024]{0,1:T(8,128)(2,1)S(1)}, bf16[128,1024]{0,1:T(8,128)(2,1)S(1)}, u32[]{:S(2)}, u32[]{:S(2)}) %collective-permute-start.1) | collective-permute-done | bytes 262176 | tf_op jit(solution)/shard_map/ppermute | solution.py:19
  126.8 3.2 fusion.60
  133.4 4.8 convert_multiply_fusion.4
  140.9 42.2 %while.180 = (s32[]{:T(128)}, bf16[8,8,512]{2,1,0:T(8,128)(2,1)S(1)}, bf16[8,8,512]{2,1,0:T(8,128)(2,1)}, bf16[8,8,512]{2,1,0:T(8,128)(2,1)}, f32[8,128,512]{2,1...) while((s32[]{:T(128)}, ...), condition=%wide.region_9.10_spmd, body=%wide.region_5.9_spmd.sunk | while | flops 12578818 | bytes 3802245 | solution.py:270
  184.4 16.9 %all-gather = bf16[64,8,512]{2,1,0:T(8,128)(2,1)S(1)} all-gather(bf16[8,8,512]{2,1,0:T(8,128)(2,1)} %copy-done.16), channel_id=2, replica_groups=mesh['section'=4,'ctx'=8] {'ctx'}, dimensions={0}, use_global_device_ids=true | all-gather | bytes 589824 | tf_op jit(solution)/shard_map/all_gather | solution.py:33
  201.3 15.2 %all-gather.2 = bf16[64,8,512]{2,1,0:T(8,128)(2,1)S(1)} all-gather(bf16[8,8,512]{2,1,0:T(8,128)(2,1)} %get-tuple-element.1000), channel_id=4, replica_groups=mesh['section'=4,'ctx'=8] {'ctx'}, dimensions={0}, use_global_device_ids=true | all-gather | bytes 589824 | tf_op jit(solution)/shard_map/all_gather | solution.py:33
  217.0 15.9 %all-gather.1 = bf16[64,8,512]{2,1,0:T(8,128)(2,1)} all-gather(bf16[8,8,512]{2,1,0:T(8,128)(2,1)} %get-tuple-element.998), channel_id=3, replica_groups=mesh['section'=4,'ctx'=8] {'ctx'}, dimensions={0}, use_global_device_ids=true | all-gather | bytes 589824 | tf_op jit(solution)/shard_map/all_gather | solution.py:33
  233.0 3.2 copy.238
  236.9 406.6 %while.185 = (s32[]{:T(128)}, f32[8,128,512]{2,1,0:T(8,128)}, f32[8,128,512]{2,1,0:T(8,128)}, f32[8,128,512]{2,1,0:T(8,128)}, f32[8,8,512]{2,1,0:T(8,128)}, /*in...) while((s32[]{:T(128)}, f32[8,128,512]{2,1,0:T(8,128)}, ...), condition=%wide.region_30.31_spmd, body=%wide.region_14.30_spmd.sunk | while | flops 14146568 | bytes 15898745 | solution.py:282
  241.9 12.3 %while.186 = (s32[]{:T(128)}, f32[8,512]{1,0:T(8,128)S(1)}, f32[4,32,8,512]{3,2,1,0:T(8,128)}, f32[4,8,512]{2,1,0:T(8,128)S(1)}, f32[4,32,512]{2,1,0:T(8,128)S(1...) while((s32[]{:T(128)}, f32[8,512]{1,0:T(8,128)S(1)}, ...), condition=%wide.region_20.20_spmd, body=%wide.region_15.19_spmd.sunk | while | flops 6389506 | bytes 3251873 | solution.py:153
  257.7 23.4 %while.187 = (s32[]{:T(128)}, f32[8,512]{1,0:T(8,128)S(1)}, f32[8,512]{1,0:T(8,128)S(1)}, f32[4,32,512]{2,1,0:T(8,128)}, f32[4,32,8]{2,1,0:T(8,128)}, /*index=5*...) while((s32[]{:T(128)}, f32[8,512]{1,0:T(8,128)S(1)}, ...), condition=%wide.region_28.28_spmd.clone, body=%wide.region_21.27_spmd.clone.sunk | while | flops 7167748 | bytes 4088035 | solution.py:178
  292.7 12.3 %while.186 = (s32[]{:T(128)}, f32[8,512]{1,0:T(8,128)S(1)}, f32[4,32,8,512]{3,2,1,0:T(8,128)}, f32[4,8,512]{2,1,0:T(8,128)S(1)}, f32[4,32,512]{2,1,0:T(8,128)S(1...) while((s32[]{:T(128)}, f32[8,512]{1,0:T(8,128)S(1)}, ...), condition=%wide.region_20.20_spmd, body=%wide.region_15.19_spmd.sunk | while | flops 6389506 | bytes 3251873 | solution.py:153
  308.5 23.4 %while.187 = (s32[]{:T(128)}, f32[8,512]{1,0:T(8,128)S(1)}, f32[8,512]{1,0:T(8,128)S(1)}, f32[4,32,512]{2,1,0:T(8,128)}, f32[4,32,8]{2,1,0:T(8,128)}, /*index=5*...) while((s32[]{:T(128)}, f32[8,512]{1,0:T(8,128)S(1)}, ...), condition=%wide.region_28.28_spmd.clone, body=%wide.region_21.27_spmd.clone.sunk | while | flops 7167748 | bytes 4088035 | solution.py:178
  343.6 12.3 %while.186 = (s32[]{:T(128)}, f32[8,512]{1,0:T(8,128)S(1)}, f32[4,32,8,512]{3,2,1,0:T(8,128)}, f32[4,8,512]{2,1,0:T(8,128)S(1)}, f32[4,32,512]{2,1,0:T(8,128)S(1...) while((s32[]{:T(128)}, f32[8,512]{1,0:T(8,128)S(1)}, ...), condition=%wide.region_20.20_spmd, body=%wide.region_15.19_spmd.sunk | while | flops 6389506 | bytes 3251873 | solution.py:153
  359.3 23.4 %while.187 = (s32[]{:T(128)}, f32[8,512]{1,0:T(8,128)S(1)}, f32[8,512]{1,0:T(8,128)S(1)}, f32[4,32,512]{2,1,0:T(8,128)}, f32[4,32,8]{2,1,0:T(8,128)}, /*index=5*...) while((s32[]{:T(128)}, f32[8,512]{1,0:T(8,128)S(1)}, ...), condition=%wide.region_28.28_spmd.clone, body=%wide.region_21.27_spmd.clone.sunk | while | flops 7167748 | bytes 4088035 | solution.py:178
  394.4 12.3 %while.186 = (s32[]{:T(128)}, f32[8,512]{1,0:T(8,128)S(1)}, f32[4,32,8,512]{3,2,1,0:T(8,128)}, f32[4,8,512]{2,1,0:T(8,128)S(1)}, f32[4,32,512]{2,1,0:T(8,128)S(1...) while((s32[]{:T(128)}, f32[8,512]{1,0:T(8,128)S(1)}, ...), condition=%wide.region_20.20_spmd, body=%wide.region_15.19_spmd.sunk | while | flops 6389506 | bytes 3251873 | solution.py:153
  410.2 23.4 %while.187 = (s32[]{:T(128)}, f32[8,512]{1,0:T(8,128)S(1)}, f32[8,512]{1,0:T(8,128)S(1)}, f32[4,32,512]{2,1,0:T(8,128)}, f32[4,32,8]{2,1,0:T(8,128)}, /*index=5*...) while((s32[]{:T(128)}, f32[8,512]{1,0:T(8,128)S(1)}, ...), condition=%wide.region_28.28_spmd.clone, body=%wide.region_21.27_spmd.clone.sunk | while | flops 7167748 | bytes 4088035 | solution.py:178
  445.2 12.3 %while.186 = (s32[]{:T(128)}, f32[8,512]{1,0:T(8,128)S(1)}, f32[4,32,8,512]{3,2,1,0:T(8,128)}, f32[4,8,512]{2,1,0:T(8,128)S(1)}, f32[4,32,512]{2,1,0:T(8,128)S(1...) while((s32[]{:T(128)}, f32[8,512]{1,0:T(8,128)S(1)}, ...), condition=%wide.region_20.20_spmd, body=%wide.region_15.19_spmd.sunk | while | flops 6389506 | bytes 3251873 | solution.py:153
  461.0 23.4 %while.187 = (s32[]{:T(128)}, f32[8,512]{1,0:T(8,128)S(1)}, f32[8,512]{1,0:T(8,128)S(1)}, f32[4,32,512]{2,1,0:T(8,128)}, f32[4,32,8]{2,1,0:T(8,128)}, /*index=5*...) while((s32[]{:T(128)}, f32[8,512]{1,0:T(8,128)S(1)}, ...), condition=%wide.region_28.28_spmd.clone, body=%wide.region_21.27_spmd.clone.sunk | while | flops 7167748 | bytes 4088035 | solution.py:178
  496.0 12.3 %while.186 = (s32[]{:T(128)}, f32[8,512]{1,0:T(8,128)S(1)}, f32[4,32,8,512]{3,2,1,0:T(8,128)}, f32[4,8,512]{2,1,0:T(8,128)S(1)}, f32[4,32,512]{2,1,0:T(8,128)S(1...) while((s32[]{:T(128)}, f32[8,512]{1,0:T(8,128)S(1)}, ...), condition=%wide.region_20.20_spmd, body=%wide.region_15.19_spmd.sunk | while | flops 6389506 | bytes 3251873 | solution.py:153
  511.8 23.4 %while.187 = (s32[]{:T(128)}, f32[8,512]{1,0:T(8,128)S(1)}, f32[8,512]{1,0:T(8,128)S(1)}, f32[4,32,512]{2,1,0:T(8,128)}, f32[4,32,8]{2,1,0:T(8,128)}, /*index=5*...) while((s32[]{:T(128)}, f32[8,512]{1,0:T(8,128)S(1)}, ...), condition=%wide.region_28.28_spmd.clone, body=%wide.region_21.27_spmd.clone.sunk | while | flops 7167748 | bytes 4088035 | solution.py:178
  546.9 12.3 %while.186 = (s32[]{:T(128)}, f32[8,512]{1,0:T(8,128)S(1)}, f32[4,32,8,512]{3,2,1,0:T(8,128)}, f32[4,8,512]{2,1,0:T(8,128)S(1)}, f32[4,32,512]{2,1,0:T(8,128)S(1...) while((s32[]{:T(128)}, f32[8,512]{1,0:T(8,128)S(1)}, ...), condition=%wide.region_20.20_spmd, body=%wide.region_15.19_spmd.sunk | while | flops 6389506 | bytes 3251873 | solution.py:153
  562.7 23.4 %while.187 = (s32[]{:T(128)}, f32[8,512]{1,0:T(8,128)S(1)}, f32[8,512]{1,0:T(8,128)S(1)}, f32[4,32,512]{2,1,0:T(8,128)}, f32[4,32,8]{2,1,0:T(8,128)}, /*index=5*...) while((s32[]{:T(128)}, f32[8,512]{1,0:T(8,128)S(1)}, ...), condition=%wide.region_28.28_spmd.clone, body=%wide.region_21.27_spmd.clone.sunk | while | flops 7167748 | bytes 4088035 | solution.py:178
  597.7 12.3 %while.186 = (s32[]{:T(128)}, f32[8,512]{1,0:T(8,128)S(1)}, f32[4,32,8,512]{3,2,1,0:T(8,128)}, f32[4,8,512]{2,1,0:T(8,128)S(1)}, f32[4,32,512]{2,1,0:T(8,128)S(1...) while((s32[]{:T(128)}, f32[8,512]{1,0:T(8,128)S(1)}, ...), condition=%wide.region_20.20_spmd, body=%wide.region_15.19_spmd.sunk | while | flops 6389506 | bytes 3251873 | solution.py:153
  613.5 23.4 %while.187 = (s32[]{:T(128)}, f32[8,512]{1,0:T(8,128)S(1)}, f32[8,512]{1,0:T(8,128)S(1)}, f32[4,32,512]{2,1,0:T(8,128)}, f32[4,32,8]{2,1,0:T(8,128)}, /*index=5*...) while((s32[]{:T(128)}, f32[8,512]{1,0:T(8,128)S(1)}, ...), condition=%wide.region_28.28_spmd.clone, body=%wide.region_21.27_spmd.clone.sunk | while | flops 7167748 | bytes 4088035 | solution.py:178
  649.5 50.8 %while.179 = (s32[]{:T(128)}, bf16[4,128,4,128]{1,3,2,0:T(8,128)(2,1)S(1)}, bf16[4,128,4,128]{3,1,2,0:T(8,128)(2,1)}, bf16[4,128,4,1024]{3,1,2,0:T(8,128)(2,1)},...) while((s32[]{:T(128)}, ...), condition=%wide.region_4.5_spmd, body=%wide.region_0.4_spmd.sunk | while | flops 545324160 | bytes 18240196 | solution.py:233
  700.3 4.2 fusion.70
  712.1 4.1 copy.202
  719.0 4.1 copy.211
  731.0 4.0 fusion.72
  735.1 35.5 %all-reduce = (bf16[1,4,4096]{2,1,0:T(4,128)(2,1)S(1)}, bf16[1,4096]{1,0:T(2,128)(2,1)S(1)}, bf16[1,4096]{1,0:T(2,128)(2,1)S(1)}) all-reduce(bf16[1,4,4096]{2,1,0:T(4,128)(2,1)S(1)} %maximum_bitcast_fusion, bf16[1,4096]{1,0:T(2,128)(2,1)S(1)} %broadcast_in_dim.190, ...), channel_id=1, replica_groups=mesh['section'=4,'ctx'=8] {'ctx'}, use_global_device_ids=true, to_apply=%region_38.39 | all-reduce | flops 24576 | bytes 98304 | tf_op jit(solution)/shard_map/psum | solution.py:320
  (1347 shorter events, 560.1 us)
Async XLA Ops:
  7.2 16.6 %copy-start.35 = (f32[1,4096]{1,0:T(1,128)S(1)}, f32[1,4096]{1,0:T(1,128)}, u32[]{:S(2)}) copy-start(f32[1,4096]{1,0:T(1,128)} %param.33) | copy-start | bytes 49156
  7.2 17.9 %copy-start.20 = (bf16[1,128,2048]{2,1,0:T(8,128)(2,1)S(1)}, bf16[1,128,2048]{2,1,0:T(8,128)(2,1)}, u32[]{:S(2)}) copy-start(bf16[1,128,2048]{2,1,0:T(8,128)(2,1)} %param.28) | copy-start | bytes 1572868
  7.2 642.3 %all-gather.5.cloned.1.call-start = ((), (), s32[]{:S(2)}) async-start(), calls=%async_computation.1 | async-start | bytes 2359296 | tf_op jit(solution)/shard_map/all_gather | solution.py:222
  7.2 113.9 %collective-permute-start.3 = (bf16[3,128,4096]{2,1,0:T(8,128)(2,1)}, bf16[3,128,4096]{2,1,0:T(8,128)(2,1)}, u32[]{:S(2)}, u32[]{:S(2)}) collective-permute-start(bf16[3,128,4096]{2,1,0:T(8,128)(2,1)} %bitcast.473), channel_id=1, source_target_pairs={{24,0},{0,8},{8,16},{16,24},{25,1},{1,9},{9,17},{17,25},{26,2},{2,... | collective-permute-start | bytes 9437192 | tf_op jit(solution)/shard_map/ppermute | solution.py:19
  10.2 123.2 %collective-permute-start.6 = (bf16[128,4096]{1,0:T(8,128)(2,1)}, bf16[128,4096]{1,0:T(8,128)(2,1)S(1)}, u32[]{:S(2)}, u32[]{:S(2)}) collective-permute-start(bf16[128,4096]{1,0:T(8,128)(2,1)} %bitcast.474), channel_id=1, source_target_pairs={{8,0},{16,8},{24,16},{0,24},{9,1},{17,9},{25,17},{1,25},{10,2},{18... | collective-permute-start | bytes 3145736 | tf_op jit(solution)/shard_map/ppermute | solution.py:19
  12.1 91.4 %collective-permute-start.4 = (bf16[128,16]{1,0:T(8,128)(2,1)S(1)}, bf16[128,16]{1,0:T(8,128)(2,1)S(1)}, u32[]{:S(2)}, u32[]{:S(2)}) collective-permute-start(bf16[128,16]{1,0:T(8,128)(2,1)S(1)} %bitcast.470), channel_id=1, source_target_pairs={{24,0},{0,8},{8,16},{16,24},{25,1},{1,9},{9,17},{17,25},{26,2},{2,... | collective-permute-start | bytes 12296 | tf_op jit(solution)/shard_map/ppermute | solution.py:19
  15.2 634.3 %collective-permute-start = (bf16[128,2048]{0,1:T(8,128)(2,1)}, bf16[128,2048]{0,1:T(8,128)(2,1)}, u32[]{:S(2)}, u32[]{:S(2)}) collective-permute-start(bf16[128,2048]{0,1:T(8,128)(2,1)} %bitcast.50), channel_id=1, source_target_pairs={{24,0},{0,8},{8,16},{16,24},{25,1},{1,9},{9,17},{17,25},{26,2},{2,... | collective-permute-start | bytes 1572872 | tf_op jit(solution)/shard_map/ppermute | solution.py:19
  18.7 101.7 %collective-permute-start.1 = (bf16[128,1024]{0,1:T(8,128)(2,1)S(1)}, bf16[128,1024]{0,1:T(8,128)(2,1)S(1)}, u32[]{:S(2)}, u32[]{:S(2)}) collective-permute-start(bf16[128,1024]{0,1:T(8,128)(2,1)S(1)} %bitcast.456), channel_id=1, source_target_pairs={{24,0},{0,8},{8,16},{16,24},{25,1},{1,9},{9,17},{17,25},{26,2},{2,... | collective-permute-start | bytes 786440 | tf_op jit(solution)/shard_map/ppermute | solution.py:19
  103.5 545.9 %collective-permute-start.2 = (bf16[128,2048]{0,1:T(8,128)(2,1)}, bf16[128,2048]{0,1:T(8,128)(2,1)}, u32[]{:S(2)}, u32[]{:S(2)}) collective-permute-start(bf16[128,2048]{0,1:T(8,128)(2,1)} %bitcast.54), channel_id=1, source_target_pairs={{8,0},{16,8},{24,16},{0,24},{9,1},{17,9},{25,17},{1,25},{10,2},{18... | collective-permute-start | bytes 1572872 | tf_op jit(solution)/shard_map/ppermute | solution.py:19
  121.1 654.4 %all-reduce.3.cloned.1.call-start = ((), (), s32[]{:S(2)}) async-start(), calls=%async_computation.3 | async-start | bytes 131072 | tf_op jit(solution)/shard_map/psum | solution.py:322
  122.0 8.0 %collective-permute-start.5 = (bf16[3,4096]{1,0:T(4,128)(2,1)S(1)}, bf16[3,4096]{1,0:T(4,128)(2,1)S(1)}, u32[]{:S(2)}, u32[]{:S(2)}) collective-permute-start(bf16[3,4096]{1,0:T(4,128)(2,1)S(1)} %slice_bitcast_fusion.9), channel_id=1, source_target_pairs={{0,1},{1,2},{2,3},{3,4},{4,5},{5,6},{6,7},{8,9},{9,10},{10,11},{11... | collective-permute-start | bytes 73736 | tf_op jit(solution)/shard_map/ppermute | solution.py:25
  281.1 6.6 copy-start.9
  281.1 6.6 copy-start.11
  331.9 6.6 copy-start.9
  331.9 6.6 copy-start.11
  382.7 6.6 copy-start.9
  382.8 6.6 copy-start.11
  433.6 6.6 copy-start.9
  433.6 6.6 copy-start.11
  484.4 6.6 copy-start.9
  484.4 6.6 copy-start.11
  535.2 6.6 copy-start.9
  535.2 6.6 copy-start.11
  586.1 6.6 copy-start.9
  586.1 6.6 copy-start.11
  636.9 6.6 copy-start.9
  636.9 6.6 copy-start.11
  649.4 130.3 %reduce-scatter.2.cloned.1.call-start = ((), (), s32[]{:S(2)}) async-start(), calls=%async_computation.2 | async-start | bytes 2359296 | tf_op jit(solution)/shard_map/reduce_scatter | solution.py:239
  710.6 61.9 %collective-permute-start.7 = (bf16[3,4096]{1,0:T(4,128)(2,1)S(1)}, bf16[3,4096]{1,0:T(4,128)(2,1)S(1)}, u32[]{:S(2)}, u32[]{:S(2)}) collective-permute-start(bf16[3,4096]{1,0:T(4,128)(2,1)S(1)} %slice.222), channel_id=1, source_target_pairs={{1,0},{2,1},{3,2},{4,3},{5,4},{6,5},{7,6},{9,8},{10,9},{11,10},{12... | collective-permute-start | bytes 73736 | tf_op jit(solution)/shard_map/ppermute | solution.py:25
  731.0 41.5 %copy-start.29 = (f32[1,1,4096]{2,1,0:T(1,128)S(1)}, f32[1,1,4096]{2,1,0:T(1,128)}, u32[]{:S(2)}) copy-start(f32[1,1,4096]{2,1,0:T(1,128)} %get-tuple-element.1421) | copy-start | bytes 49156
  731.0 41.5 %copy-start.31 = (f32[1,1,4096]{2,1,0:T(1,128)S(1)}, f32[1,1,4096]{2,1,0:T(1,128)}, u32[]{:S(2)}) copy-start(f32[1,1,4096]{2,1,0:T(1,128)} %get-tuple-element.1422) | copy-start | bytes 49156
  731.0 41.5 %copy-start.33 = (f32[1,1,4096]{2,1,0:T(1,128)S(1)}, f32[1,1,4096]{2,1,0:T(1,128)}, u32[]{:S(2)}) copy-start(f32[1,1,4096]{2,1,0:T(1,128)} %get-tuple-element.1423) | copy-start | bytes 49156
  (65 other events, 163.8 us)
Sparse Core Ops, SparseCore 0:
  121.2 31.6 all-gather.4
  649.5 59.6 all-reduce.2
  711.6 39.0 reduce-scatter.1
where the time goes:
time: 803 us; the launch traced here: 788 us
  local copies, waits for them, and re-layouts  381 us (47%)
  other arithmetic  164 us (20%)
  waiting for transfers between devices  91.7 us (11%)
  blocking collectives  83.5 us (10%)
  matrix products  28.9 us (4%)
  between operations  14.3 us (2%)
  starting transfers between devices  13.1 us (2%)
  loops' own time  11.8 us (1%)
    ppermute x6, waiting for transfers between devices, shifted(): return lax.ppermute(block, axis, route)  91.6 us
    all_gather x3, blocking collectives, carried_in(): lax.all_gather(a.astype(kind), axis)  48 us
    dynamic_update_slice x160, local copies, waits for them, and re-layouts, full_pass(): lax.scan(forward_sub, start_state, (in_subs(step_k), in_subs(moved_k), in...  41.2 us
    psum x1, blocking collectives, body(): lax.psum(tap_grad.astype(jnp.bfloat16), 'ctx').astype(jnp.float32)  35.5 us
    slice x32, local copies, waits for them, and re-layouts, backward_sub(): before = jnp.concatenate([prior_p[None], states_p[:-1]], axis=0)  34.4 us
    another operation x32, other arithmetic, backward_sub(): lax.cumsum(jnp.exp(log_decay) * source, axis=0, reverse=True)  32.7 us
    dynamic_update_slice x32, other arithmetic, full_pass(): lax.scan(forward_sub, start_state, (in_subs(step_k), in_subs(moved_k), in...  29.4 us
    dynamic_slice x24, local copies, waits for them, and re-layouts, body(): lax.map(partial(end_states, b_proj=b_proj, c_proj=c_proj), (step_blocks,...  29 us
  transfers between devices with their start and end apart: 11, of which 2 were waited for; matrix products, arithmetic and copies ran while one was open for 71% of the time, Pallas kernels for 0%

commit v1 on v0

--- a/solution.py
+++ b/solution.py
@@ -1,9 +1,9 @@
-from functools import partial
-
 import jax
 import jax.numpy as jnp
 from jax import lax
 from jax.sharding import PartitionSpec as P
+from jax.experimental import pallas as pl
+from jax.experimental.pallas import tpu as pltpu
 
 C = 4096
 NSTATE = 8
@@ -25,54 +25,17 @@
     return lax.ppermute(shard, axis, pairs)
 
 
-def carried_in(shard, axis, join, neutral, backward):
-    count = lax.axis_size(axis)
-    place = lax.axis_index(axis)
-    ahead = count - 1 - place if backward else place
-    gathered = jax.tree.map(
-        lambda a, kind: lax.all_gather(a.astype(kind), axis), shard, (jnp.bfloat16, jnp.bfloat16)
-    )
-    state = jax.tree.map(lambda a, e: jnp.zeros_like(a) + jnp.asarray(e, a.dtype), shard, neutral)
-
-    def one(hop, state):
-        source = count - 1 - hop if backward else hop
-        return join(
-            state,
-            jax.tree.map(
-                lambda a, own: lax.dynamic_index_in_dim(a, source, 0, False).astype(own.dtype),
-                gathered,
-                shard,
-            ),
-        )
-
-    return lax.fori_loop(0, ahead, one, state)
-
-
 def shortened(shard):
 
     def short(part):
         return part.astype(jnp.bfloat16) if part.dtype == jnp.float32 else part
 
     return jax.tree.map(short, shard)
-
-
-def combine_pairs(earlier, later):
-    return (earlier[0] * later[0], later[0] * earlier[1] + later[1])
 
 
 def silu_slope(value):
     sigmoid_v = jax.nn.sigmoid(value)
     return sigmoid_v * (1.0 + value * (1.0 - sigmoid_v))
-
-
-def to_blocks(matrix, block_width):
-    return matrix.reshape(matrix.shape[0], matrix.shape[1] // block_width, block_width).transpose(
-        1, 0, 2
-    )
-
-
-def from_blocks(stacked):
-    return stacked.transpose(1, 0, 2).reshape(stacked.shape[1], stacked.shape[0] * stacked.shape[2])
 
 
 def attention_group(group_index, query_heads, grad_heads, key_whole, first_row, softmax_scale):
@@ -119,84 +82,182 @@
     return jnp.stack([key_grad, value_grad], axis=1)
 
 
-def end_states(pieces_in, b_proj, c_proj):
-    step_k, moved_k, drive_k, rate_k = pieces_in
-    cumulative = lax.cumsum(step_k, axis=0)
-    whole_sum = cumulative[-1]
-    ahead = jnp.exp((whole_sum[None, :] - cumulative)[:, None, :] * rate_k[None])
-    state_end = jnp.sum(ahead * b_proj[:, :, None] * moved_k[:, None, :], axis=0)
-    behind = jnp.exp(cumulative[:, None, :] * rate_k[None])
-    adjoint_end = jnp.sum(behind * c_proj[:, :, None] * drive_k[:, None, :], axis=0)
-    return (jnp.exp(whole_sum[None, :] * rate_k), state_end, adjoint_end)
-
-
-def full_pass(pieces_in, b_proj, c_proj, sub_length):
-    step_k, moved_k, drive_k, rate_k, inner_k, skip_k, start_state, start_adjoint = pieces_in
-    row_count = step_k.shape[0]
-    block_width = step_k.shape[1]
-    splits = row_count // sub_length
-
-    def in_subs(matrix):
-        return matrix.reshape(splits, sub_length, matrix.shape[1])
-
-    def forward_sub(running, pieces_sub):
-        step_p, moved_p, b_part, c_part, drive_p = pieces_sub
-        log_decay = lax.cumsum(step_p, axis=0)[:, None, :] * rate_k[None]
-        inflow = b_part[:, :, None] * moved_p[:, None, :]
-        states = jnp.exp(log_decay) * (
-            running[None] + lax.cumsum(jnp.exp(-log_decay) * inflow, axis=0)
-        )
-        mixed_part = jnp.sum(states * c_part[:, :, None], axis=1)
-        c_part_grad = jnp.sum(states * drive_p[:, None, :], axis=2)
-        return (states[-1], (states, running, mixed_part, c_part_grad))
-
-    _, (states, priors, mixed_parts, c_grads) = lax.scan(
-        forward_sub,
-        start_state,
-        (in_subs(step_k), in_subs(moved_k), in_subs(b_proj), in_subs(c_proj), in_subs(drive_k)),
-    )
-
-    def backward_sub(carry, pieces_sub):
-        running, rate_total = carry
-        step_p, drive_p, c_part, b_part, moved_p, states_p, prior_p = pieces_sub
-        log_decay = lax.cumsum(step_p, axis=0)[:, None, :] * rate_k[None]
-        source = c_part[:, :, None] * drive_p[:, None, :]
-        tail_sum = (
-            lax.cumsum(jnp.exp(log_decay) * source, axis=0, reverse=True)
-            + jnp.exp(log_decay[-1])[None] * running
-        )
-        adjoints = jnp.exp(-log_decay) * tail_sum
-        before = jnp.concatenate([prior_p[None], states_p[:-1]], axis=0)
-        through = adjoints * before * jnp.exp(step_p[:, None, :] * rate_k[None])
-        adjoint_b = jnp.sum(adjoints * b_part[:, :, None], axis=1)
-        b_part_grad = jnp.sum(adjoints * moved_p[:, None, :], axis=2)
-        through_rate = jnp.sum(through * rate_k[None], axis=1)
-        rate_total = rate_total + jnp.sum(through * step_p[:, None, :], axis=0)
-        return ((tail_sum[0], rate_total), (adjoint_b, b_part_grad, through_rate))
-
-    start_carry = (start_adjoint, jnp.zeros_like(start_adjoint))
-    (_, rate_grad), (adjoint_parts, b_grads, through_parts) = lax.scan(
-        backward_sub,
-        start_carry,
-        (
-            in_subs(step_k),
-            in_subs(drive_k),
-            in_subs(c_proj),
-            in_subs(b_proj),
-            in_subs(moved_k),
-            states,
-            priors,
+LANES = 128
+ROWS = 8
+
+
+def fold_rows(parts):
+    rows = lax.broadcasted_iota(jnp.int32, parts[0].shape, 0)
+
+    def pair(first, second, k):
+        low = (rows & k) == 0
+        kept = jnp.where(low, first, second)
+        moved = jnp.where(low, second, first)
+        if k == 4:
+            swapped = pltpu.roll(moved, 4, 0)
+        else:
+            swapped = jnp.where(low, pltpu.roll(moved, ROWS - k, 0), pltpu.roll(moved, k, 0))
+        return kept + swapped
+
+    stage = [pair(parts[n], parts[n + 4], 4) for n in range(4)]
+    stage = [pair(stage[n], stage[n + 2], 2) for n in range(2)]
+    return pair(stage[0], stage[1], 1)
+
+
+def summary_kernel(b_ref, c_ref, dt_ref, u_ref, gy_ref, a_ref, s_ref, g_ref):
+    steps = dt_ref.shape[0]
+    count = a_ref.shape[0]
+    rates = [a_ref[n] for n in range(count)]
+
+    def advance(t, carry):
+        state, decay, adjoint = carry
+        dt = dt_ref[t]
+        moved = u_ref[t]
+        drive = gy_ref[t]
+        next_state, next_decay, next_adjoint = [], [], []
+        for n in range(count):
+            factor = jnp.exp(dt * rates[n])
+            next_state.append(factor * state[n] + b_ref[t * count + n] * moved)
+            d = decay[n] * factor
+            next_decay.append(d)
+            next_adjoint.append(adjoint[n] + (c_ref[t * count + n] * d) * drive)
+        return (tuple(next_state), tuple(next_decay), tuple(next_adjoint))
+
+    zeros = tuple(jnp.zeros_like(r) for r in rates)
+    ones = tuple(jnp.ones_like(r) for r in rates)
+    state, _, adjoint = lax.fori_loop(0, steps, advance, (zeros, ones, zeros), unroll=2)
+    for n in range(count):
+        s_ref[n] = state[n]
+        g_ref[n] = adjoint[n]
+
+
+def full_kernel(
+    b_ref, c_ref, dt_ref, u_ref, gy_ref, a_ref, hin_ref, gin_ref,
+    y_ref, gu_ref, gdt_ref, ga_ref, gc_ref, gb_ref, hist_ref,
+):
+    steps = dt_ref.shape[0]
+    count = a_ref.shape[0]
+    rates = [a_ref[n] for n in range(count)]
+    start = tuple(hin_ref[n] for n in range(count))
+    for n in range(count):
+        hist_ref[0, n] = start[n]
+
+    def forward(t, state):
+        dt = dt_ref[t]
+        moved = u_ref[t]
+        drive = gy_ref[t]
+        mixed = None
+        parts = []
+        next_state = []
+        for n in range(count):
+            factor = jnp.exp(dt * rates[n])
+            h = factor * state[n] + b_ref[t * count + n] * moved
+            hist_ref[t + 1, n] = h
+            term = c_ref[t * count + n] * h
+            mixed = term if mixed is None else mixed + term
+            parts.append(h * drive)
+            next_state.append(h)
+        y_ref[t] = mixed
+        gc_ref[t] = fold_rows(parts)
+        return tuple(next_state)
+
+    lax.fori_loop(0, steps, forward, start, unroll=2)
+
+    def backward(i, carry):
+        t = steps - 1 - i
+        pending, rate_acc = carry
+        dt = dt_ref[t]
+        moved = u_ref[t]
+        drive = gy_ref[t]
+        step_acc = None
+        moved_acc = None
+        parts = []
+        next_pending = []
+        next_rate = []
+        for n in range(count):
+            factor = jnp.exp(dt * rates[n])
+            adj = c_ref[t * count + n] * drive + pending[n]
+            through = adj * factor * hist_ref[t, n]
+            x1 = through * rates[n]
+            step_acc = x1 if step_acc is None else step_acc + x1
+            next_rate.append(rate_acc[n] + through * dt)
+            x2 = b_ref[t * count + n] * adj
+            moved_acc = x2 if moved_acc is None else moved_acc + x2
+            parts.append(adj * moved)
+            next_pending.append(factor * adj)
+        gdt_ref[t] = step_acc
+        gu_ref[t] = moved_acc
+        gb_ref[t] = fold_rows(parts)
+        return (tuple(next_pending), tuple(next_rate))
+
+    pending0 = tuple(gin_ref[n] for n in range(count))
+    zeros = tuple(jnp.zeros_like(r) for r in rates)
+    _, rate_acc = lax.fori_loop(0, steps, backward, (pending0, zeros), unroll=2)
+    for n in range(count):
+        ga_ref[n] = rate_acc[n]
+
+
+def scan_specs(steps, count, blocks):
+    smem = pl.BlockSpec(memory_space=pltpu.SMEM)
+    rows = pl.BlockSpec((steps, ROWS, LANES), lambda j: (0, j, 0))
+    states = pl.BlockSpec((count, ROWS, LANES), lambda j: (0, j, 0))
+    return smem, rows, states
+
+
+def mamba_summary(b_flat, c_flat, dt_r, u_r, gy_r, a_r):
+    steps = dt_r.shape[0]
+    count = a_r.shape[0]
+    blocks = dt_r.shape[1] // ROWS
+    smem, rows, states = scan_specs(steps, count, blocks)
+    shape = jax.ShapeDtypeStruct(a_r.shape, jnp.float32)
+    elems = steps * count * dt_r.shape[1] * LANES
+    return pl.pallas_call(
+        summary_kernel,
+        grid=(blocks,),
+        in_specs=[smem, smem, rows, rows, rows, states],
+        out_specs=[states, states],
+        out_shape=[shape, shape],
+        cost_estimate=pl.CostEstimate(
+            flops=9 * elems, transcendentals=elems, bytes_accessed=4 * 3 * dt_r.size
         ),
-        reverse=True,
-    )
-    adjoint_b = adjoint_parts.reshape(row_count, block_width)
-    mixed_out = mixed_parts.reshape(row_count, block_width) + skip_k * inner_k
-    step_grad = through_parts.reshape(row_count, block_width) + adjoint_b * inner_k
-    inner_grad = adjoint_b * step_k + skip_k * drive_k
-    b_grad = b_grads.reshape(row_count, -1)
-    c_grad = c_grads.reshape(row_count, -1)
-    skip_grad = jnp.sum(drive_k * inner_k, axis=0)
-    return (mixed_out, step_grad, inner_grad, rate_grad, b_grad, c_grad, skip_grad)
+    )(b_flat, c_flat, dt_r, u_r, gy_r, a_r)
+
+
+def mamba_full(b_flat, c_flat, dt_r, u_r, gy_r, a_r, h_in, g_in):
+    steps = dt_r.shape[0]
+    count = a_r.shape[0]
+    blocks = dt_r.shape[1] // ROWS
+    smem, rows, states = scan_specs(steps, count, blocks)
+    folded = pl.BlockSpec((None, steps, count, LANES), lambda j: (j, 0, 0, 0))
+    row_shape = jax.ShapeDtypeStruct(dt_r.shape, jnp.float32)
+    fold_shape = jax.ShapeDtypeStruct((blocks, steps, count, LANES), jnp.float32)
+    elems = steps * count * dt_r.shape[1] * LANES
+    return pl.pallas_call(
+        full_kernel,
+        grid=(blocks,),
+        in_specs=[smem, smem, rows, rows, rows, states, states, states],
+        out_specs=[rows, rows, rows, states, folded, folded],
+        out_shape=[
+            row_shape,
+            row_shape,
+            row_shape,
+            jax.ShapeDtypeStruct(a_r.shape, jnp.float32),
+            fold_shape,
+            fold_shape,
+        ],
+        scratch_shapes=[pltpu.VMEM((steps + 1, count, ROWS, LANES), jnp.float32)],
+        cost_estimate=pl.CostEstimate(
+            flops=30 * elems, transcendentals=2 * elems, bytes_accessed=4 * 6 * dt_r.size
+        ),
+    )(b_flat, c_flat, dt_r, u_r, gy_r, a_r, h_in, g_in)
+
+
+def lanes_view(matrix):
+    return matrix.reshape(matrix.shape[0], matrix.shape[1] // LANES, LANES)
+
+
+def flat_view(stacked):
+    return stacked.reshape(stacked.shape[0], stacked.shape[1] * stacked.shape[2])
 
 
 def body(
@@ -260,45 +321,42 @@
     out_grad = mamba_grad.astype(jnp.float32)
     out_drive = out_grad * gate_act
     moved_in = step_size * inner_act
-    block_width = min(C, 512)
-    block_count = C // block_width
-    sub_length = min(row_count, 32)
-    step_blocks = to_blocks(step_size, block_width)
-    moved_blocks = to_blocks(moved_in, block_width)
-    drive_blocks = to_blocks(out_drive, block_width)
-    rate_blocks = to_blocks(decay_rate, block_width)
-    decays, state_ends, adjoint_ends = lax.map(
-        partial(end_states, b_proj=b_proj, c_proj=c_proj),
-        (step_blocks, moved_blocks, drive_blocks, rate_blocks),
-    )
-    unit_decays = jnp.ones_like(decays)
-    zero_states = jnp.zeros_like(decays)
-    _, state_in = carried_in(
-        (decays, state_ends), "ctx", combine_pairs, (unit_decays, zero_states), False
-    )
-    _, adjoint_in = carried_in(
-        (decays, adjoint_ends), "ctx", combine_pairs, (unit_decays, zero_states), True
-    )
-    results = lax.map(
-        partial(full_pass, b_proj=b_proj, c_proj=c_proj, sub_length=sub_length),
-        (
-            step_blocks,
-            moved_blocks,
-            drive_blocks,
-            rate_blocks,
-            to_blocks(inner_act, block_width),
-            skip_gain[0].reshape(block_count, block_width),
-            state_in,
-            adjoint_in,
-        ),
-    )
-    mixed_out = from_blocks(results[0])
-    step_grad = from_blocks(results[1])
-    inner_grad = from_blocks(results[2])
-    rate_grad = from_blocks(results[3])
-    b_grad = jnp.sum(results[4], axis=0)
-    c_grad = jnp.sum(results[5], axis=0)
-    skip_grad = results[6].reshape(C)
+    b_flat = b_proj.reshape(-1)
+    c_flat = c_proj.reshape(-1)
+    dt_r = lanes_view(step_size)
+    u_r = lanes_view(moved_in)
+    gy_r = lanes_view(out_drive)
+    a_r = lanes_view(decay_rate)
+    state_end, adjoint_end = mamba_summary(b_flat, c_flat, dt_r, u_r, gy_r, a_r)
+    step_total = jnp.sum(dt_r, axis=0)
+    gathered = lax.all_gather(
+        jnp.concatenate([state_end, adjoint_end, step_total[None]], axis=0), "ctx"
+    )
+    count = a_r.shape[0]
+    place = lax.axis_index("ctx")
+    devices = gathered.shape[0]
+    state_in = jnp.zeros_like(state_end)
+    adjoint_in = jnp.zeros_like(adjoint_end)
+    for other in range(devices):
+        decay = jnp.exp(a_r * gathered[other, 2 * count][None])
+        state_in = jnp.where(
+            other < place, decay * state_in + gathered[other, :count], state_in
+        )
+    for other in reversed(range(devices)):
+        decay = jnp.exp(a_r * gathered[other, 2 * count][None])
+        adjoint_in = jnp.where(
+            other > place, decay * adjoint_in + gathered[other, count : 2 * count], adjoint_in
+        )
+    y_ssm, moved_grad, step_ssm, rate_grad_r, c_fold, b_fold = mamba_full(
+        b_flat, c_flat, dt_r, u_r, gy_r, a_r, state_in, adjoint_in
+    )
+    mixed_out = flat_view(y_ssm) + skip_gain[0] * inner_act
+    step_grad = flat_view(step_ssm) + flat_view(moved_grad) * inner_act
+    inner_grad = flat_view(moved_grad) * step_size + skip_gain[0] * out_drive
+    rate_grad = flat_view(rate_grad_r)
+    b_grad = jnp.sum(b_fold, axis=(0, 3))
+    c_grad = jnp.sum(c_fold, axis=(0, 3))
+    skip_grad = jnp.sum(out_drive * inner_act, axis=0)
     mamba_out = (mixed_out * gate_act).astype(jnp.bfloat16)
     gating_grad = out_grad * mixed_out * silu_slope(gating_f)
     raw_grad = step_grad * jax.nn.sigmoid(unscaled_step.astype(jnp.float32))

time: 803 us -> 347 us (0.43); the launches traced: 788 us -> 346 us
  local copies, waits for them, and re-layouts: 381 us -> 29.1 us
  other arithmetic: 164 us -> 54.1 us
  blocking collectives: 83.5 us -> 28.4 us
  Pallas kernels: 0 us -> 38.6 us
  waiting for transfers between devices: 91.7 us -> 128 us
    mul x200 -> x1, local copies, waits for them, and re-layouts: 110 us -> 0.85 us  [body(): decay = jnp.exp(a_r * gathered[other, 2 * count][None])]
    dynamic_update_slice x200 -> x0, local copies, waits for them, and re-layouts: 78.8 us -> none  [the longest x160 41.2 us: full_pass(): lax.scan(forward_sub, start_state, (in_subs(step_k), in_subs(moved_k), in...]
    dynamic_slice x64 -> x0, local copies, waits for them, and re-layouts: 58 us -> none  [the longest x24 29 us: body(): lax.map(partial(end_states, b_proj=b_proj, c_proj=c_proj), (step_blocks,...]
    another operation x162 -> x4, other arithmetic: 53.2 us -> 0.01 us  [the longest x32 32.7 us: backward_sub(): lax.cumsum(jnp.exp(log_decay) * source, axis=0, reverse=True)]
    all_gather x3 -> x0, blocking collectives: 48 us -> none  [carried_in(): lax.all_gather(a.astype(kind), axis)]
    pallas_call x0 -> x2, Pallas kernels: none -> 38.6 us  [the longest x1 28 us: mamba_full(): pl.pallas_call(full_kernel, grid=(blocks,), in_specs=[smem, smem, rows, r...]
    slice x40 -> x0, local copies, waits for them, and re-layouts: 34.5 us -> none  [the longest x32 34.4 us: backward_sub(): before = jnp.concatenate([prior_p[None], states_p[:-1]], axis=0)]
    reduce_scatter x1, waiting for transfers between devices: 0.01 us -> 32.4 us  [body(): lax.psum_scatter(whole_term.astype(jnp.bfloat16), 'ctx', scatter_dimensio...]
  transfers between devices with their start and end apart: 11 -> 12, of which waited for: 2 -> 4; matrix products, arithmetic and copies ran while one was open for 71% -> 30% of each run, Pallas kernels for 0% -> 3%
where the time goes in v1:
time: 347 us; the launch traced here: 346 us
  waiting for transfers between devices  128 us (37%)
  other arithmetic  54.1 us (16%)
  Pallas kernels  38.6 us (11%)
  matrix products  32.3 us (9%)
  local copies, waits for them, and re-layouts  29.1 us (8%)
  blocking collectives  28.4 us (8%)
  between operations  14.2 us (4%)
  starting transfers between devices  13.2 us (4%)
  loops' own time  7.89 us (2%)
    ppermute x6, waiting for transfers between devices, shifted(): return lax.ppermute(block, axis, route)  92.3 us
    reduce_scatter x1, waiting for transfers between devices, body(): lax.psum_scatter(whole_term.astype(jnp.bfloat16), 'ctx', scatter_dimensio...  32.4 us
    psum x1, blocking collectives, body(): lax.psum(tap_grad.astype(jnp.bfloat16), 'ctx').astype(jnp.float32)  28.4 us
    pallas_call x1, Pallas kernels, mamba_full(): pl.pallas_call(full_kernel, grid=(blocks,), in_specs=[smem, smem, rows, r...  28 us
    unnamed x28, local copies, waits for them, and re-layouts  12.8 us
    pallas_call x1, Pallas kernels, mamba_summary(): pl.pallas_call(summary_kernel, grid=(blocks,), in_specs=[smem, smem, rows...  10.6 us
    ppermute x6, starting transfers between devices, shifted(): return lax.ppermute(block, axis, route)  10.1 us
    reduce_sum x1, other arithmetic, body(): jnp.sum(pre_grad * padded[offset:offset + row_count], axis=0)  9.91 us
  transfers between devices with their start and end apart: 12, of which 4 were waited for; matrix products, arithmetic and copies ran while one was open for 30% of the time, Pallas kernels for 3%

profile of v1, /device:TPU:0, one launch (start us, length us, event | category | flops | bytes accessed | tf_op | source)
XLA Modules:
  0.0 346.1 jit_solution(3007226418426304391)
XLA Ops:
  7.2 3.0 collective-permute-start.4
  12.2 2.0 copy.67
  14.3 2.4 collective-permute-start
  16.7 1.8 copy.68
  21.8 2.1 copy.69
  23.9 79.0 %collective-permute-done.3 = bf16[128,16]{0,1:T(8,128)(2,1)S(1)} collective-permute-done((bf16[128,16]{0,1:T(8,128)(2,1)}, bf16[128,16]{0,1:T(8,128)(2,1)S(1)}, u32[]{:S(2)}, u32[]{:S(2)}) %collective-permute-start.3) | collective-permute-done | bytes 4128 | tf_op jit(solution)/shard_map/ppermute | solution.py:19
  102.9 2.1 collective-permute-start.2
  106.5 13.3 %collective-permute-done.1 = bf16[128,1024]{0,1:T(8,128)(2,1)} collective-permute-done((bf16[128,1024]{0,1:T(8,128)(2,1)}, bf16[128,1024]{0,1:T(8,128)(2,1)}, u32[]{:S(2)}, u32[]{:S(2)}) %collective-permute-start.1) | collective-permute-done | bytes 262176 | tf_op jit(solution)/shard_map/ppermute | solution.py:19
  121.9 2.4 compare_select_fusion.2.dt_ref
  127.5 3.2 multiply_reduce_fusion.1
  132.3 1.7 copy.98
  134.0 1.7 copy.99
  135.7 10.6 %shard_map.177 = (f32[8,32,128]{2,1,0:T(8,128)}, f32[8,32,128]{2,1,0:T(8,128)}) custom-call(f32[1024]{0:T(1024)} %reshape.215.b_ref, f32[1024]{0:T(1024)} %reshape.217.c_ref, f32[128,32,128]{2,1,0:T(8,128)} %compare_select_fusion.2.dt_ref, f32[128,32,128]{2,1,0:T(8,128)} %bitcast.425, f32[128,32,128]{2,1,0:T(8,128)} %bitcast.427, f32[8,32,128]{2,1,0:T(8,128)} %bitcast.444), custom_call_target="tpu_custom_call" | custom-call | flops 37748736 | bytes 6291456 | tf_op jit(solution)/shard_map/pallas_call | solution.py:214
  146.2 1.7 pad_maximum_fusion.3
  148.2 3.5 %all-gather.4.cloned.1.call-done = bf16[1024,1024]{0,1:T(8,128)(2,1)} async-done(((bf16[128,1024]{0,1:T(8,128)(2,1)}), bf16[1024,1024]{0,1:T(8,128)(2,1)}) %all-gather.4.cloned.1.call-update) | async-done | bytes 2097168 | tf_op jit(solution)/shard_map/all_gather | solution.py:283
  151.7 53.2 %while.16 = (s32[]{:T(128)}, bf16[4,128,4,128]{1,3,2,0:T(8,128)(2,1)}, bf16[4,128,4,128]{3,1,2,0:T(8,128)(2,1)}, bf16[4,128,4,1024]{3,1,2,0:T(8,128)(2,1)}, bf16...) while((s32[]{:T(128)}, ...), condition=%wide.region_4.5_spmd, body=%wide.region_0.4_spmd.sunk | while | flops 545324160 | bytes 18240704 | solution.py:294
  161.5 2.4 bitcast_dynamic-update-slice_fusion.8
  174.8 2.4 bitcast_dynamic-update-slice_fusion.8
  188.2 2.4 bitcast_dynamic-update-slice_fusion.8
  201.5 2.4 bitcast_dynamic-update-slice_fusion.8
  205.0 4.1 %fusion.52 = bf16[1024,1,4,128]{3,0,2,1:T(8,128)(2,1)S(1)} fusion(bf16[4,128,4,1024]{3,1,2,0:T(8,128)(2,1)} %get-tuple-element.79, bf16[128,4,4,128]{0,3,2,1:T(8,128)(2,1)} %bitcast.18), kind=kOutput, calls=%fused_computation.104 | convolution fusion | flops 537395200 | bytes 5767168 | tf_op jit(solution)/shard_map/gtrs,tgrd->sgd/dot_general | solution.py:79
  209.0 3.7 %fusion.51 = bf16[1024,1,4,128]{3,0,2,1:T(8,128)(2,1)} fusion(bf16[4,128,4,1024]{3,1,2,0:T(8,128)(2,1)S(1)} %copy-done.9, bf16[128,4,4,128]{0,3,2,1:T(8,128)(2,1)} %bitcast.14), kind=kOutput, calls=%fused_computation.103 | convolution fusion | flops 537919488 | bytes 5767168 | tf_op jit(solution)/shard_map/gtrs,tgrd->sgd/dot_general | solution.py:76
  213.6 2.2 fusion.60.gin_ref
  215.7 2.2 fusion.76.hin_ref
  217.9 28.0 %shard_map.178 = (f32[128,32,128]{2,1,0:T(8,128)}, f32[128,32,128]{2,1,0:T(8,128)}, f32[128,32,128]{2,1,0:T(8,128)}, f32[8,32,128]{2,1,0:T(8,128)}, f32[4,128,8,...) custom-call(f32[1024]{0:T(1024)} %reshape.215.b_ref, f32[1024]{0:T(1024)} %reshape.217.c_ref, ...), custom_call_target="tpu_custom_call" | custom-call | flops 125829120 | bytes 12582912 | tf_op jit(solution)/shard_map/pallas_call | solution.py:235
  247.9 2.7 pad_maximum_fusion.2
  254.4 9.9 %multiply_reduce_fusion.5 = (bf16[4096]{0:T(1024)(128)(2,1)S(1)}, bf16[4096]{0:T(1024)(128)(2,1)S(1)}, bf16[4096]{0:T(1024)(128)(2,1)S(1)}, bf16[4096]{0:T(1024)...) fusion(f32[131,4096]{1,0:T(8,128)S(1)} %maximum_convert_fusion,, ...), kind=kLoop, calls=%fused_computation.96 | loop fusion | flops 27766784 | bytes 25223168 | tf_op jit(solution)/shard_map/reduce_sum | solution.py:373
  264.4 2.0 reduce_sum.100
  266.4 1.8 reduce_sum.101
  270.4 28.4 %all-reduce = (bf16[1,4,4096]{2,1,0:T(4,128)(2,1)S(1)}, bf16[1,4096]{1,0:T(2,128)(2,1)S(1)}, bf16[1,4096]{1,0:T(2,128)(2,1)S(1)}) all-reduce(bf16[1,4,4096]{2,1,0:T(4,128)(2,1)S(1)} %maximum_bitcast_fusion, bf16[1,4096]{1,0:T(2,128)(2,1)S(1)} %broadcast_in_dim.78, ...), channel_id=1, replica_groups=mesh['section'=4,'ctx'=8] {'ctx'}, use_global_device_ids=true, to_apply=%region_13.14 | all-reduce | flops 24576 | bytes 98304 | tf_op jit(solution)/shard_map/psum | solution.py:378
  301.7 2.0 pad_maximum_fusion
  305.2 32.4 %reduce-scatter.2.cloned.1.call-done = bf16[128,2,4,128]{3,0,2,1:T(8,128)(2,1)} async-done(((bf16[1024,2,4,128]{3,0,2,1:T(8,128)(2,1)}), bf16[128,2,4,128]{3,0,2,1:T(8,128)(2,1)}) %reduce-scatter.2.cloned.1.call-update) | async-done | bytes 262160 | tf_op jit(solution)/shard_map/reduce_scatter | solution.py:300
  (132 shorter events, 64.6 us)
Async XLA Ops:
  7.2 144.5 %all-gather.4.cloned.1.call-start = ((), (), s32[]{:S(2)}) async-start(), calls=%async_computation.1 | async-start | bytes 2359296 | tf_op jit(solution)/shard_map/all_gather | solution.py:283
  7.2 112.7 %collective-permute-start.4 = (bf16[3,128,4096]{2,1,0:T(8,128)(2,1)}, bf16[3,128,4096]{2,1,0:T(8,128)(2,1)S(1)}, u32[]{:S(2)}, u32[]{:S(2)}) collective-permute-start(bf16[3,128,4096]{2,1,0:T(8,128)(2,1)} %bitcast.450), channel_id=1, source_target_pairs={{24,0},{0,8},{8,16},{16,24},{25,1},{1,9},{9,17},{17,25},{26,2},{2,... | collective-permute-start | bytes 9437192 | tf_op jit(solution)/shard_map/ppermute | solution.py:19
  10.2 115.7 %collective-permute-start.6 = (bf16[128,4096]{1,0:T(8,128)(2,1)}, bf16[128,4096]{1,0:T(8,128)(2,1)}, u32[]{:S(2)}, u32[]{:S(2)}) collective-permute-start(bf16[128,4096]{1,0:T(8,128)(2,1)} %bitcast.451), channel_id=1, source_target_pairs={{8,0},{16,8},{24,16},{0,24},{9,1},{17,9},{25,17},{1,25},{10,2},{18... | collective-permute-start | bytes 3145736 | tf_op jit(solution)/shard_map/ppermute | solution.py:19
  11.2 91.6 %collective-permute-start.3 = (bf16[128,16]{0,1:T(8,128)(2,1)}, bf16[128,16]{0,1:T(8,128)(2,1)S(1)}, u32[]{:S(2)}, u32[]{:S(2)}) collective-permute-start(bf16[128,16]{0,1:T(8,128)(2,1)} %bitcast.452), channel_id=1, source_target_pairs={{24,0},{0,8},{8,16},{16,24},{25,1},{1,9},{9,17},{17,25},{26,2},{2,... | collective-permute-start | bytes 12296 | tf_op jit(solution)/shard_map/ppermute | solution.py:19
  14.3 133.9 %collective-permute-start = (bf16[128,2048]{0,1:T(8,128)(2,1)}, bf16[128,2048]{0,1:T(8,128)(2,1)}, u32[]{:S(2)}, u32[]{:S(2)}) collective-permute-start(bf16[128,2048]{0,1:T(8,128)(2,1)} %bitcast.430), channel_id=1, source_target_pairs={{24,0},{0,8},{8,16},{16,24},{25,1},{1,9},{9,17},{17,25},{26,2},{2,... | collective-permute-start | bytes 1572872 | tf_op jit(solution)/shard_map/ppermute | solution.py:19
  18.5 101.4 %collective-permute-start.1 = (bf16[128,1024]{0,1:T(8,128)(2,1)}, bf16[128,1024]{0,1:T(8,128)(2,1)}, u32[]{:S(2)}, u32[]{:S(2)}) collective-permute-start(bf16[128,1024]{0,1:T(8,128)(2,1)} %bitcast.15), channel_id=1, source_target_pairs={{24,0},{0,8},{8,16},{16,24},{25,1},{1,9},{9,17},{17,25},{26,2},{2,... | collective-permute-start | bytes 786440 | tf_op jit(solution)/shard_map/ppermute | solution.py:19
  102.9 45.3 %collective-permute-start.2 = (bf16[128,2048]{0,1:T(8,128)(2,1)}, bf16[128,2048]{0,1:T(8,128)(2,1)}, u32[]{:S(2)}, u32[]{:S(2)}) collective-permute-start(bf16[128,2048]{0,1:T(8,128)(2,1)} %bitcast.433), channel_id=1, source_target_pairs={{8,0},{16,8},{24,16},{0,24},{9,1},{17,9},{25,17},{1,25},{10,2},{18... | collective-permute-start | bytes 1572872 | tf_op jit(solution)/shard_map/ppermute | solution.py:19
  119.9 92.9 %all-gather.6.cloned.1.call-start = ((), (), s32[]{:S(2)}) async-start(), calls=%async_computation.4 | async-start | bytes 2506752 | tf_op jit(solution)/shard_map/all_gather | solution.py:332
  119.9 4.4 %copy-start.1 = (bf16[3,128,4096]{2,1,0:T(8,128)(2,1)}, bf16[3,128,4096]{2,1,0:T(8,128)(2,1)S(1)}, u32[]{:S(2)}) copy-start(bf16[3,128,4096]{2,1,0:T(8,128)(2,1)S(1)} %collective-permute-done.4) | copy-start | bytes 9437188
  120.0 5.7 %collective-permute-start.5 = (bf16[3,4096]{1,0:T(4,128)(2,1)S(1)}, bf16[3,4096]{1,0:T(4,128)(2,1)S(1)}, u32[]{:S(2)}, u32[]{:S(2)}) collective-permute-start(bf16[3,4096]{1,0:T(4,128)(2,1)S(1)} %slice_bitcast_fusion.24), channel_id=1, source_target_pairs={{0,1},{1,2},{2,3},{3,4},{4,5},{5,6},{6,7},{8,9},{9,10},{10,11},{11... | collective-permute-start | bytes 73736 | tf_op jit(solution)/shard_map/ppermute | solution.py:25
  125.6 1.9 copy-start.2
  125.6 1.9 copy-start.8
  130.7 1.6 copy-start
  148.0 155.7 %all-reduce.3.cloned.1.call-start = ((), (), s32[]{:S(2)}) async-start(), calls=%async_computation.3 | async-start | bytes 131072 | tf_op jit(solution)/shard_map/psum | solution.py:380
  205.0 4.1 %copy-start.9 = (bf16[4,128,4,1024]{3,1,2,0:T(8,128)(2,1)S(1)}, bf16[4,128,4,1024]{3,1,2,0:T(8,128)(2,1)}, u32[]{:S(2)}) copy-start(bf16[4,128,4,1024]{3,1,2,0:T(8,128)(2,1)} %get-tuple-element.78) | copy-start | bytes 12582916
  217.9 28.0 %copy-start.6 = (f32[1,8,4096]{2,1,0:T(8,128)S(1)}, f32[1,8,4096]{2,1,0:T(8,128)}, u32[]{:S(2)}) copy-start(f32[1,8,4096]{2,1,0:T(8,128)} %param.20) | copy-start | bytes 393220
  247.6 90.0 %reduce-scatter.2.cloned.1.call-start = ((), (), s32[]{:S(2)}) async-start(), calls=%async_computation.2 | async-start | bytes 2359296 | tf_op jit(solution)/shard_map/reduce_scatter | solution.py:300
  250.6 2.7 copy-start.5
  250.6 3.7 %copy-start.7 = (f32[1,4096]{1,0:T(1,128)S(1)}, f32[1,4096]{1,0:T(1,128)}, u32[]{:S(2)}) copy-start(f32[1,4096]{1,0:T(1,128)} %param.21) | copy-start | bytes 49156
  264.4 4.0 %copy-start.3 = (f32[128,4096]{1,0:T(8,128)S(1)}, f32[128,4096]{1,0:T(8,128)}, u32[]{:S(2)}) copy-start(f32[128,4096]{1,0:T(8,128)} %get-tuple-element.187) | copy-start | bytes 6291460
  268.4 32.3 %collective-permute-start.7 = (bf16[3,4096]{1,0:T(4,128)(2,1)S(1)}, bf16[3,4096]{1,0:T(4,128)(2,1)S(1)}, u32[]{:S(2)}, u32[]{:S(2)}) collective-permute-start(bf16[3,4096]{1,0:T(4,128)(2,1)S(1)} %slice.428), channel_id=1, source_target_pairs={{1,0},{2,1},{3,2},{4,3},{5,4},{6,5},{7,6},{9,8},{10,9},{11,10},{12... | collective-permute-start | bytes 73736 | tf_op jit(solution)/shard_map/ppermute | solution.py:25
  298.8 2.9 copy-start.4
Sparse Core Ops, SparseCore 0:
  120.0 31.6 all-gather.3
  153.3 29.2 all-gather.5
  247.7 52.6 all-reduce.2
  302.7 34.8 reduce-scatter.1

commit v2 on v1

--- a/solution.py
+++ b/solution.py
@@ -260,60 +260,20 @@
     return stacked.reshape(stacked.shape[0], stacked.shape[1] * stacked.shape[2])
 
 
-def body(
-    queries,
-    keys_values,
-    mix_in,
-    proj_bc,
-    attn_cot,
-    mamba_cot,
-    conv_weight,
-    conv_bias,
-    a_log,
-    skip_gain,
-):
-    query_in, pair_in, mixture, proj_in = shifted(
-        (queries[0], keys_values[0], mix_in[0], proj_bc[0]), "section", 1
-    )
-    attn_grad, mamba_grad = shifted((attn_cot[0], mamba_cot[0]), "section", -1)
-    row_count = query_in.shape[0]
-    group_size = HEADS // KVHEADS
-    softmax_scale = HDIM ** (-0.5)
-    first_row = lax.axis_index("ctx") * row_count
-    pairs_whole = lax.all_gather(pair_in, "ctx", axis=0, tiled=True)
-    seq_length = pairs_whole.shape[0]
-    key_whole = pairs_whole.reshape(seq_length, 2, KVHEADS, HDIM)
-    query_heads = query_in.reshape(row_count, KVHEADS, group_size, HDIM)
-    grad_heads = attn_grad.reshape(row_count, KVHEADS, group_size, HDIM)
-
-    def per_group(group_index):
-        return attention_group(
-            group_index, query_heads, grad_heads, key_whole, first_row, softmax_scale
-        )
-
-    outputs, query_grads, probs_all, score_all = lax.map(
-        per_group, jnp.arange(KVHEADS, dtype=jnp.int32)
-    )
-    attn_out = outputs.transpose(1, 0, 2, 3).reshape(row_count, HEADS * HDIM)
-    query_out = query_grads.transpose(1, 0, 2, 3).reshape(row_count, HEADS * HDIM)
-    whole_term = key_terms(probs_all, score_all, query_heads, grad_heads, softmax_scale)
-    key_sum = lax.psum_scatter(
-        whole_term.astype(jnp.bfloat16), "ctx", scatter_dimension=0, tiled=True
-    )
-    pair_out = key_sum.reshape(row_count, 2 * KVHEADS * HDIM)
+def mamba_chunk(mixture, mamba_grad, proj_in, conv_taps, conv_shift, log_rates, direct_gain):
     signal = mixture[0]
     gating = mixture[1]
     unscaled_step = mixture[2]
+    row_count = signal.shape[0]
     conv_rows = KCONV - 1
     rim_rows = passed_along(signal[row_count - conv_rows :], "ctx", 1)
     padded = jnp.concatenate([rim_rows, signal], axis=0).astype(jnp.float32)
-    conv_taps = conv_weight[0]
-    preact = conv_bias[0]
+    preact = conv_shift
     for offset in range(KCONV):
         preact = preact + conv_taps[offset] * padded[offset : offset + row_count]
     inner_act = jax.nn.silu(preact)
     step_size = jax.nn.softplus(unscaled_step.astype(jnp.float32))
-    decay_rate = -jnp.exp(a_log[0])
+    decay_rate = -jnp.exp(log_rates)
     b_proj = proj_in[:, :NSTATE].astype(jnp.float32)
     c_proj = proj_in[:, NSTATE:].astype(jnp.float32)
     gating_f = gating.astype(jnp.float32)
@@ -350,9 +310,9 @@
     y_ssm, moved_grad, step_ssm, rate_grad_r, c_fold, b_fold = mamba_full(
         b_flat, c_flat, dt_r, u_r, gy_r, a_r, state_in, adjoint_in
     )
-    mixed_out = flat_view(y_ssm) + skip_gain[0] * inner_act
+    mixed_out = flat_view(y_ssm) + direct_gain * inner_act
     step_grad = flat_view(step_ssm) + flat_view(moved_grad) * inner_act
-    inner_grad = flat_view(moved_grad) * step_size + skip_gain[0] * out_drive
+    inner_grad = flat_view(moved_grad) * step_size + direct_gain * out_drive
     rate_grad = flat_view(rate_grad_r)
     b_grad = jnp.sum(b_fold, axis=(0, 3))
     c_grad = jnp.sum(c_fold, axis=(0, 3))
@@ -374,13 +334,97 @@
     )
     bias_grad = jnp.sum(pre_grad, axis=0)
     log_grad = rate_grad * decay_rate
-    tap_sum, bias_sum, log_sum, skip_sum = (
-        lax.psum(tap_grad.astype(jnp.bfloat16), "ctx").astype(jnp.float32),
-        lax.psum(bias_grad.astype(jnp.bfloat16), "ctx").astype(jnp.float32),
-        lax.psum(log_grad.astype(jnp.bfloat16), "ctx").astype(jnp.float32),
-        lax.psum(skip_grad.astype(jnp.bfloat16), "ctx").astype(jnp.float32),
-    )
+    weight_parts = jnp.concatenate(
+        [tap_grad, bias_grad[None], log_grad, skip_grad[None]], axis=0
+    ).astype(jnp.bfloat16)
     mix_out = jnp.stack([signal_grad, gating_grad, raw_grad]).astype(jnp.bfloat16)
+    return mamba_out, mix_out, b_grad, c_grad, weight_parts
+
+
+def body(
+    queries,
+    keys_values,
+    mix_in,
+    proj_bc,
+    attn_cot,
+    mamba_cot,
+    conv_weight,
+    conv_bias,
+    a_log,
+    skip_gain,
+):
+    query_in, pair_in, proj_in = shifted((queries[0], keys_values[0], proj_bc[0]), "section", 1)
+    attn_grad = shifted(attn_cot[0], "section", -1)
+    mix_local, cot_local, _, _, _ = lax.optimization_barrier(
+        (mix_in[0], mamba_cot[0], query_in, pair_in, attn_grad)
+    )
+    channels = mix_local.shape[-1]
+    pieces = 2 if channels % (2 * ROWS * LANES) == 0 else 1
+    width = channels // pieces
+    arrived = []
+    for piece in range(pieces):
+        mix_part = mix_local[:, :, piece * width : (piece + 1) * width]
+        cot_part = cot_local[:, piece * width : (piece + 1) * width]
+        if arrived:
+            mix_part, cot_part, _, _ = lax.optimization_barrier(
+                (mix_part, cot_part) + arrived[-1]
+            )
+        arrived.append((shifted(mix_part, "section", 1), shifted(cot_part, "section", -1)))
+    row_count = query_in.shape[0]
+    group_size = HEADS // KVHEADS
+    softmax_scale = HDIM ** (-0.5)
+    first_row = lax.axis_index("ctx") * row_count
+    pairs_whole = lax.all_gather(pair_in, "ctx", axis=0, tiled=True)
+    seq_length = pairs_whole.shape[0]
+    key_whole = pairs_whole.reshape(seq_length, 2, KVHEADS, HDIM)
+    query_heads = query_in.reshape(row_count, KVHEADS, group_size, HDIM)
+    grad_heads = attn_grad.reshape(row_count, KVHEADS, group_size, HDIM)
+
+    def per_group(group_index):
+        return attention_group(
+            group_index, query_heads, grad_heads, key_whole, first_row, softmax_scale
+        )
+
+    outputs, query_grads, probs_all, score_all = lax.map(
+        per_group, jnp.arange(KVHEADS, dtype=jnp.int32)
+    )
+    attn_out = outputs.transpose(1, 0, 2, 3).reshape(row_count, HEADS * HDIM)
+    query_out = query_grads.transpose(1, 0, 2, 3).reshape(row_count, HEADS * HDIM)
+    whole_term = key_terms(probs_all, score_all, query_heads, grad_heads, softmax_scale)
+    first_mix, first_cot, attn_out, query_out, whole_term = lax.optimization_barrier(
+        arrived[0] + (attn_out, query_out, whole_term)
+    )
+    arrived[0] = (first_mix, first_cot)
+    key_sum = lax.psum_scatter(
+        whole_term.astype(jnp.bfloat16), "ctx", scatter_dimension=0, tiled=True
+    )
+    pair_out = key_sum.reshape(row_count, 2 * KVHEADS * HDIM)
+    results = []
+    for piece, (mix_part, cot_part) in enumerate(arrived):
+        cut = slice(piece * width, (piece + 1) * width)
+        results.append(
+            mamba_chunk(
+                mix_part,
+                cot_part,
+                proj_in,
+                conv_weight[0][:, cut],
+                conv_bias[0][cut],
+                a_log[0][:, cut],
+                skip_gain[0][cut],
+            )
+        )
+    mamba_out = jnp.concatenate([r[0] for r in results], axis=1)
+    mix_out = jnp.concatenate([r[1] for r in results], axis=2)
+    b_grad = sum(r[2] for r in results)
+    c_grad = sum(r[3] for r in results)
+    weight_parts = jnp.concatenate([r[4] for r in results], axis=1)
+    weight_sum = jnp.sum(lax.all_gather(weight_parts, "ctx").astype(jnp.float32), axis=0)
+    taps = conv_weight.shape[1]
+    states = a_log.shape[1]
+    tap_sum = weight_sum[:taps]
+    bias_sum = weight_sum[taps]
+    log_sum = weight_sum[taps + 1 : taps + 1 + states]
+    skip_sum = weight_sum[taps + 1 + states]
     proj_out = jnp.concatenate([b_grad, c_grad], axis=1).astype(jnp.bfloat16)
     return (
         attn_out[None],

time: 347 us -> 353 us (1.017)
  waiting for transfers between devices: 128 us -> 105 us
  local copies, waits for them, and re-layouts: 29.1 us -> 45.3 us
  other arithmetic: 54.1 us -> 66.2 us
  blocking collectives: 28.4 us -> 19.9 us
  Pallas kernels: 38.6 us -> 43.4 us
  starting transfers between devices: 13.2 us -> 17 us
    reduce_scatter x1, waiting for transfers between devices: 32.4 us -> 0.01 us  [body(): lax.psum_scatter(whole_term.astype(jnp.bfloat16), 'ctx', scatter_dimensio...]
    psum x1 -> x0, blocking collectives: 28.4 us -> none  [body(): lax.psum(tap_grad.astype(jnp.bfloat16), 'ctx').astype(jnp.float32)]
    all_gather x0 -> x1, blocking collectives: none -> 19.9 us  [body(): lax.all_gather(weight_parts, 'ctx').astype(jnp.float32)]
    ppermute x6 -> x8, waiting for transfers between devices: 92.3 us -> 105 us  [shifted(): return lax.ppermute(block, axis, route)]
    reduce_sum x5 -> x11, other arithmetic: 18.1 us -> 24.5 us  [the longest x2 10.6 us: mamba_chunk(): jnp.sum(pre_grad * padded[offset:offset + row_count], axis=0)]
    slice x3 -> x10, local copies, waits for them, and re-layouts: 1.11 us -> 7.39 us  [the longest x1 2.49 us: body(): mix_part = mix_local[:, :, piece * width:(piece + 1) * width]]
    reshape x4 -> x7, local copies, waits for them, and re-layouts: 1.57 us -> 6.52 us  [the longest x1 2.22 us: body(): query_grads.transpose(1, 0, 2, 3).reshape(row_count, HEADS * HDIM)]
    select_n x3 -> x6, other arithmetic: 6.75 us -> 10.3 us  [the longest x2 3.63 us: mamba_chunk(): jnp.where(other > place, decay * adjoint_in + gathered[other, count:2 * c...]
  transfers between devices with their start and end apart: 12 -> 16, of which waited for: 4 -> 4; matrix products, arithmetic and copies ran while one was open for 30% -> 38% of each run, Pallas kernels for 3% -> 12%
where the time goes in v2:
time: 353 us; the launch traced here: 351 us
  waiting for transfers between devices  105 us (30%)
  other arithmetic  66.2 us (19%)
  local copies, waits for them, and re-layouts  45.3 us (13%)
  Pallas kernels  43.4 us (12%)
  matrix products  31.3 us (9%)
  blocking collectives  19.9 us (6%)
  starting transfers between devices  17 us (5%)
  between operations  14.7 us (4%)
  loops' own time  7.91 us (2%)
    ppermute x8, waiting for transfers between devices, shifted(): return lax.ppermute(block, axis, route)  105 us
    pallas_call x2, Pallas kernels, mamba_full(): pl.pallas_call(full_kernel, grid=(blocks,), in_specs=[smem, smem, rows, r...  30.9 us
    all_gather x1, blocking collectives, body(): lax.all_gather(weight_parts, 'ctx').astype(jnp.float32)  19.9 us
    pallas_call x2, Pallas kernels, mamba_summary(): pl.pallas_call(summary_kernel, grid=(blocks,), in_specs=[smem, smem, rows...  12.5 us
    ppermute x8, starting transfers between devices, shifted(): return lax.ppermute(block, axis, route)  11.3 us
    unnamed x116, local copies, waits for them, and re-layouts  10.7 us
    reduce_sum x2, other arithmetic, mamba_chunk(): jnp.sum(pre_grad * padded[offset:offset + row_count], axis=0)  10.6 us
    dot_general x4, matrix products, attention_group(): jnp.einsum('trd,sd->trs', grad_g, value_rows, preferred_element_type=jnp....  9.67 us
  transfers between devices with their start and end apart: 16, of which 4 were waited for; matrix products, arithmetic and copies ran while one was open for 38% of the time, Pallas kernels for 12%

profile of v2, /device:TPU:0, one launch (start us, length us, event | category | flops | bytes accessed | tf_op | source)
XLA Modules:
  0.0 350.8 jit_solution(3877248290989915677)
XLA Ops:
  8.6 3.0 collective-permute-start
  15.2 26.1 %collective-permute-done.1 = bf16[128,1024]{0,1:T(8,128)(2,1)S(1)} collective-permute-done((bf16[128,1024]{0,1:T(8,128)(2,1)S(1)}, bf16[128,1024]{0,1:T(8,128)(2,1)S(1)}, u32[]{:S(2)}, u32[]{:S(2)}) %collective-permute-start.1) | collective-permute-done | bytes 262176 | tf_op jit(solution)/shard_map/ppermute | solution.py:19
  41.3 2.5 fusion.173
  45.6 2.1 collective-permute-start.4
  48.0 43.6 %collective-permute-done.4 = bf16[128,2048]{1,0:T(8,128)(2,1)S(1)} collective-permute-done((bf16[128,2048]{1,0:T(8,128)(2,1)S(1)}, bf16[128,2048]{1,0:T(8,128)(2,1)S(1)}, u32[]{:S(2)}, u32[]{:S(2)}) %collective-permute-start.4) | collective-permute-done | bytes 524320 | tf_op jit(solution)/shard_map/ppermute | solution.py:19
  96.7 2.3 collective-permute-start.9
  99.0 31.6 %collective-permute-done.7 = bf16[3,128,2048]{2,1,0:T(8,128)(2,1)S(1)} collective-permute-done((bf16[3,128,2048]{2,1,0:T(8,128)(2,1)S(1)}, bf16[3,128,2048]{2,1,0:T(8,128)(2,1)S(1)}, u32[]{:S(2)}, u32[]{:S(2)}) %collective-permute-start.7) | collective-permute-done | bytes 1572896 | tf_op jit(solution)/shard_map/ppermute | solution.py:19
  134.6 3.7 %collective-permute-done.9 = bf16[128,2048]{1,0:T(8,128)(2,1)S(1)} collective-permute-done((bf16[128,2048]{1,0:T(8,128)(2,1)}, bf16[128,2048]{1,0:T(8,128)(2,1)S(1)}, u32[]{:S(2)}, u32[]{:S(2)}) %collective-permute-start.9) | collective-permute-done | bytes 524320 | tf_op jit(solution)/shard_map/ppermute | solution.py:19
  138.4 2.8 multiply_reduce_fusion.1
  145.4 6.3 %shard_map.179 = (f32[8,16,128]{2,1,0:T(8,128)}, f32[8,16,128]{2,1,0:T(8,128)}) custom-call(f32[1024]{0:T(1024)} %reshape.223.b_ref, f32[1024]{0:T(1024)} %reshape.225.c_ref, f32[128,16,128]{2,1,0:T(8,128)} %compare_select_fusion.2.dt_ref, f32[128,16,128]{2,1,0:T(8,128)} %bitcast.708, f32[128,16,128]{2,1,0:T(8,128)} %bitcast.710, ...), custom_call_target="tpu_custom_call" | custom-call | flops 18874368 | bytes 3145728 | tf_op jit(solution)/shard_map/pallas_call | solution.py:214
  153.5 53.2 %while.16 = (s32[]{:T(128)}, bf16[4,128,4,128]{1,3,2,0:T(8,128)(2,1)}, bf16[4,128,4,128]{3,1,2,0:T(8,128)(2,1)}, bf16[4,128,4,1024]{3,1,2,0:T(8,128)(2,1)}, bf16...) while((s32[]{:T(128)}, ...), condition=%wide.region_4.5_spmd, body=%wide.region_0.4_spmd.sunk | while | flops 545324160 | bytes 18240704 | solution.py:388
  163.3 2.4 bitcast_dynamic-update-slice_fusion.8
  176.6 2.4 bitcast_dynamic-update-slice_fusion.8
  189.9 2.4 bitcast_dynamic-update-slice_fusion.8
  203.1 2.5 bitcast_dynamic-update-slice_fusion.8
  206.7 4.1 %convolution_bitcast_fusion = bf16[1024,1,4,128]{3,0,2,1:T(8,128)(2,1)S(1)} fusion(bf16[4,128,4,1024]{3,1,2,0:T(8,128)(2,1)} %get-tuple-element.95, bf16[128,4,4,128]{0,3,2,1:T(8,128)(2,1)} %bitcast.20), kind=kOutput, calls=%fused_computation.51 | convolution fusion | flops 536870912 | bytes 5767168 | tf_op jit(solution)/shard_map/gtrs,tgrd->sgd/dot_general | solution.py:79
  210.8 2.7 fusion.10
  214.6 2.2 reshape.203
  216.8 2.0 copy.94
  218.9 2.8 pad_maximum_fusion
  226.9 2.3 fusion.71
  229.3 2.6 multiply_reduce_fusion.6
  232.0 2.2 multiply_bitcast_fusion.1
  236.5 6.3 %shard_map.177 = (f32[8,16,128]{2,1,0:T(8,128)}, f32[8,16,128]{2,1,0:T(8,128)}) custom-call(f32[1024]{0:T(1024)} %reshape.223.b_ref, f32[1024]{0:T(1024)} %reshape.225.c_ref, f32[128,16,128]{2,1,0:T(8,128)} %compare_select_fusion.5.dt_ref, f32[128,16,128]{2,1,0:T(8,128)} %bitcast.712, f32[128,16,128]{2,1,0:T(8,128)} %bitcast.714, ...), custom_call_target="tpu_custom_call" | custom-call | flops 18874368 | bytes 3145728 | tf_op jit(solution)/shard_map/pallas_call | solution.py:214
  250.4 15.4 %shard_map.180 = (f32[128,16,128]{2,1,0:T(8,128)}, f32[128,16,128]{2,1,0:T(8,128)}, f32[128,16,128]{2,1,0:T(8,128)}, f32[8,16,128]{2,1,0:T(8,128)}, f32[2,128,8,...) custom-call(f32[1024]{0:T(1024)} %reshape.223.b_ref, f32[1024]{0:T(1024)} %reshape.225.c_ref, ...), custom_call_target="tpu_custom_call" | custom-call | flops 62914560 | bytes 6291456 | tf_op jit(solution)/shard_map/pallas_call | solution.py:235
  265.8 5.3 %multiply_reduce_fusion.2 = (bf16[2048]{0:T(1024)(128)(2,1)S(1)}, bf16[2048]{0:T(1024)(128)(2,1)S(1)}, bf16[2048]{0:T(1024)(128)(2,1)S(1)}, bf16[2048]{0:T(1024)...) fusion(f32[131,2048]{1,0:T(8,128)S(1)} %maximum_convert_fusion., ...), kind=kLoop, calls=%fused_computation.156 | loop fusion | flops 13883392 | bytes 12611584 | tf_op jit(solution)/shard_map/reduce_sum | solution.py:333
  277.6 2.1 reduce_sum.192
  282.7 1.8 fusion.135.gin_ref
  286.3 15.5 %shard_map.178 = (f32[128,16,128]{2,1,0:T(8,128)}, f32[128,16,128]{2,1,0:T(8,128)}, f32[128,16,128]{2,1,0:T(8,128)}, f32[8,16,128]{2,1,0:T(8,128)}, f32[2,128,8,...) custom-call(f32[1024]{0:T(1024)} %reshape.223.b_ref, f32[1024]{0:T(1024)} %reshape.225.c_ref, ...), custom_call_target="tpu_custom_call" | custom-call | flops 62914560 | bytes 6291456 | tf_op jit(solution)/shard_map/pallas_call | solution.py:235
  301.9 5.3 %multiply_reduce_fusion.7 = (bf16[2048]{0:T(1024)(128)(2,1)S(1)}, bf16[2048]{0:T(1024)(128)(2,1)S(1)}, bf16[2048]{0:T(1024)(128)(2,1)S(1)}, bf16[2048]{0:T(1024)...) fusion(f32[131,2048]{1,0:T(8,128)S(1)} %maximum_convert_fusion,, ...), kind=kLoop, calls=%fused_computation.161 | loop fusion | flops 13883392 | bytes 12611584 | tf_op jit(solution)/shard_map/reduce_sum | solution.py:333
  309.4 19.9 %all-gather.3 = bf16[8,14,4096]{2,1,0:T(8,128)(2,1)S(1)} all-gather(bf16[1,14,4096]{2,1,0:T(8,128)(2,1)S(1)} %maximum_bitcast_fusion.2), channel_id=4, replica_groups=mesh['section'=4,'ctx'=8] {'ctx'}, dimensions={0}, use_global_device_ids=true | all-gather | bytes 1032192 | tf_op jit(solution)/shard_map/all_gather | solution.py:421
  329.5 2.2 reduce_sum.191
  (263 shorter events, 99.9 us)
Async XLA Ops:
  7.2 146.3 %all-gather.8.cloned.1.call-start = ((), (), s32[]{:S(2)}) async-start(), calls=%async_computation.1 | async-start | bytes 2359296 | tf_op jit(solution)/shard_map/all_gather | solution.py:377
  8.6 32.7 %collective-permute-start = (bf16[128,2048]{0,1:T(8,128)(2,1)S(1)}, bf16[128,2048]{0,1:T(8,128)(2,1)S(1)}, u32[]{:S(2)}, u32[]{:S(2)}) collective-permute-start(bf16[128,2048]{0,1:T(8,128)(2,1)S(1)} %bitcast.722), channel_id=1, source_target_pairs={{24,0},{0,8},{8,16},{16,24},{25,1},{1,9},{9,17},{17,25},{26,2},{2,... | collective-permute-start | bytes 1572872 | tf_op jit(solution)/shard_map/ppermute | solution.py:19
  12.9 28.4 %collective-permute-start.2 = (bf16[128,2048]{0,1:T(8,128)(2,1)S(1)}, bf16[128,2048]{0,1:T(8,128)(2,1)}, u32[]{:S(2)}, u32[]{:S(2)}) collective-permute-start(bf16[128,2048]{0,1:T(8,128)(2,1)S(1)} %bitcast.723), channel_id=1, source_target_pairs={{8,0},{16,8},{24,16},{0,24},{9,1},{17,9},{25,17},{1,25},{10,2},{18... | collective-permute-start | bytes 1572872 | tf_op jit(solution)/shard_map/ppermute | solution.py:19
  14.1 27.2 %collective-permute-start.1 = (bf16[128,1024]{0,1:T(8,128)(2,1)S(1)}, bf16[128,1024]{0,1:T(8,128)(2,1)S(1)}, u32[]{:S(2)}, u32[]{:S(2)}) collective-permute-start(bf16[128,1024]{0,1:T(8,128)(2,1)S(1)} %bitcast.726), channel_id=1, source_target_pairs={{24,0},{0,8},{8,16},{16,24},{25,1},{1,9},{9,17},{17,25},{26,2},{2,... | collective-permute-start | bytes 786440 | tf_op jit(solution)/shard_map/ppermute | solution.py:19
  43.8 49.2 %copy-start.50 = (f32[1,4096]{1,0:T(1,128)S(1)}, f32[1,4096]{1,0:T(1,128)}, u32[]{:S(2)}) copy-start(f32[1,4096]{1,0:T(1,128)} %param.19) | copy-start | bytes 49156
  43.9 49.9 %copy-start.21 = (f32[1,8,4096]{2,1,0:T(8,128)S(1)}, f32[1,8,4096]{2,1,0:T(8,128)}, u32[]{:S(2)}) copy-start(f32[1,8,4096]{2,1,0:T(8,128)} %param.20) | copy-start | bytes 393220
  43.9 49.9 %copy-start.40 = (f32[1,4,4096]{2,1,0:T(4,128)S(1)}, f32[1,4,4096]{2,1,0:T(4,128)}, u32[]{:S(2)}) copy-start(f32[1,4,4096]{2,1,0:T(4,128)} %param.18) | copy-start | bytes 196612
  43.9 47.7 %collective-permute-start.3 = (bf16[3,128,2048]{2,1,0:T(8,128)(2,1)S(1)}, bf16[3,128,2048]{2,1,0:T(8,128)(2,1)}, u32[]{:S(2)}, u32[]{:S(2)}) collective-permute-start(bf16[3,128,2048]{2,1,0:T(8,128)(2,1)S(1)} %get-tuple-element.244), channel_id=1, source_target_pairs={{24,0},{0,8},{8,16},{16,24},{25,1},{1,9},{9,17},{17,25},{26,2},{2,... | collective-permute-start | bytes 4718600 | tf_op jit(solution)/shard_map/ppermute | solution.py:19
  45.6 46.0 %collective-permute-start.4 = (bf16[128,2048]{1,0:T(8,128)(2,1)S(1)}, bf16[128,2048]{1,0:T(8,128)(2,1)S(1)}, u32[]{:S(2)}, u32[]{:S(2)}) collective-permute-start(bf16[128,2048]{1,0:T(8,128)(2,1)S(1)} %get-tuple-element.268), channel_id=1, source_target_pairs={{8,0},{16,8},{24,16},{0,24},{9,1},{17,9},{25,17},{1,25},{10,2},{18... | collective-permute-start | bytes 1572872 | tf_op jit(solution)/shard_map/ppermute | solution.py:19
  47.8 47.4 %collective-permute-start.5 = (bf16[128,16]{0,1:T(8,128)(2,1)}, bf16[128,16]{0,1:T(8,128)(2,1)S(1)}, u32[]{:S(2)}, u32[]{:S(2)}) collective-permute-start(bf16[128,16]{0,1:T(8,128)(2,1)} %bitcast.33), channel_id=1, source_target_pairs={{24,0},{0,8},{8,16},{16,24},{25,1},{1,9},{9,17},{17,25},{26,2},{2,... | collective-permute-start | bytes 12296 | tf_op jit(solution)/shard_map/ppermute | solution.py:19
  92.4 38.2 %collective-permute-start.7 = (bf16[3,128,2048]{2,1,0:T(8,128)(2,1)S(1)}, bf16[3,128,2048]{2,1,0:T(8,128)(2,1)S(1)}, u32[]{:S(2)}, u32[]{:S(2)}) collective-permute-start(bf16[3,128,2048]{2,1,0:T(8,128)(2,1)S(1)} %get-tuple-element.102), channel_id=1, source_target_pairs={{24,0},{0,8},{8,16},{16,24},{25,1},{1,9},{9,17},{17,25},{26,2},{2,... | collective-permute-start | bytes 4718600 | tf_op jit(solution)/shard_map/ppermute | solution.py:19
  93.7 152.3 %all-gather.12.cloned.1.call-start = ((), (), s32[]{:S(2)}) async-start(), calls=%async_computation.4 | async-start | bytes 1253376 | tf_op jit(solution)/shard_map/all_gather | solution.py:292
  94.4 44.0 %copy-start.30 = (f32[1,2048]{1,0:T(1,128)}, f32[1,2048]{1,0:T(1,128)S(1)}, u32[]{:S(2)}) copy-start(f32[1,2048]{1,0:T(1,128)S(1)} %get-tuple-element.276) | copy-start | bytes 24580
  94.4 44.0 %copy-start.32 = (f32[1,2048]{1,0:T(1,128)}, f32[1,2048]{1,0:T(1,128)S(1)}, u32[]{:S(2)}) copy-start(f32[1,2048]{1,0:T(1,128)S(1)} %get-tuple-element.277) | copy-start | bytes 24580
  94.4 44.0 %copy-start.34 = (f32[1,2048]{1,0:T(1,128)}, f32[1,2048]{1,0:T(1,128)S(1)}, u32[]{:S(2)}) copy-start(f32[1,2048]{1,0:T(1,128)S(1)} %get-tuple-element.278) | copy-start | bytes 24580
  94.4 44.0 %copy-start.36 = (f32[1,2048]{1,0:T(1,128)}, f32[1,2048]{1,0:T(1,128)S(1)}, u32[]{:S(2)}) copy-start(f32[1,2048]{1,0:T(1,128)S(1)} %get-tuple-element.279) | copy-start | bytes 24580
  96.7 41.7 %collective-permute-start.9 = (bf16[128,2048]{1,0:T(8,128)(2,1)}, bf16[128,2048]{1,0:T(8,128)(2,1)S(1)}, u32[]{:S(2)}, u32[]{:S(2)}) collective-permute-start(bf16[128,2048]{1,0:T(8,128)(2,1)} %get-tuple-element.103), channel_id=1, source_target_pairs={{8,0},{16,8},{24,16},{0,24},{9,1},{17,9},{25,17},{1,25},{10,2},{18... | collective-permute-start | bytes 1572872 | tf_op jit(solution)/shard_map/ppermute | solution.py:19
  130.7 3.8 %collective-permute-start.8 = (bf16[3,2048]{1,0:T(4,128)(2,1)S(1)}, bf16[3,2048]{1,0:T(4,128)(2,1)S(1)}, u32[]{:S(2)}, u32[]{:S(2)}) collective-permute-start(bf16[3,2048]{1,0:T(4,128)(2,1)S(1)} %slice_bitcast_fusion.43), channel_id=1, source_target_pairs={{0,1},{1,2},{2,3},{3,4},{4,5},{5,6},{6,7},{8,9},{9,10},{10,11},{11... | collective-permute-start | bytes 36872 | tf_op jit(solution)/shard_map/ppermute | solution.py:25
  153.2 128.6 %all-gather.10.cloned.1.call-start = ((), (), s32[]{:S(2)}) async-start(), calls=%async_computation.3 | async-start | bytes 1253376 | tf_op jit(solution)/shard_map/all_gather | solution.py:292
  223.8 5.4 %collective-permute-start.6 = (bf16[3,2048]{1,0:T(4,128)(2,1)S(1)}, bf16[3,2048]{1,0:T(4,128)(2,1)S(1)}, u32[]{:S(2)}, u32[]{:S(2)}) collective-permute-start(bf16[3,2048]{1,0:T(4,128)(2,1)S(1)} %slice_bitcast_fusion.44), channel_id=1, source_target_pairs={{0,1},{1,2},{2,3},{3,4},{4,5},{5,6},{6,7},{8,9},{9,10},{10,11},{11... | collective-permute-start | bytes 36872 | tf_op jit(solution)/shard_map/ppermute | solution.py:25
  244.3 97.9 %reduce-scatter.2.cloned.1.call-start = ((), (), s32[]{:S(2)}) async-start(), calls=%async_computation.2 | async-start | bytes 2359296 | tf_op jit(solution)/shard_map/reduce_scatter | solution.py:398
  250.4 15.4 %copy-start.42 = (f32[1,2048]{1,0:T(1,128)S(1)}, f32[1,2048]{1,0:T(1,128)}, u32[]{:S(2)}) copy-start(f32[1,2048]{1,0:T(1,128)} %get-tuple-element.286) | copy-start | bytes 24580
  265.8 7.6 %copy-start.48 = (bf16[2048]{0:T(1024)(128)(2,1)S(1)}, bf16[2048]{0:T(1024)(128)(2,1)}, u32[]{:S(2)}) copy-start(bf16[2048]{0:T(1024)(128)(2,1)} %get-tuple-element.224) | copy-start | bytes 12292
  271.1 8.6 %copy-start.17 = (f32[2,128,8,128]{3,2,1,0:T(8,128)S(1)}, f32[2,128,8,128]{3,2,1,0:T(8,128)}, u32[]{:S(2)}) copy-start(f32[2,128,8,128]{3,2,1,0:T(8,128)} %get-tuple-element.116) | copy-start | bytes 3145732
  272.1 8.4 %collective-permute-start.11 = (bf16[3,2048]{1,0:T(4,128)(2,1)S(1)}, bf16[3,2048]{1,0:T(4,128)(2,1)S(1)}, u32[]{:S(2)}, u32[]{:S(2)}) collective-permute-start(bf16[3,2048]{1,0:T(4,128)(2,1)S(1)} %slice.917), channel_id=1, source_target_pairs={{1,0},{2,1},{3,2},{4,3},{5,4},{6,5},{7,6},{9,8},{10,9},{11,10},{12... | collective-permute-start | bytes 36872 | tf_op jit(solution)/shard_map/ppermute | solution.py:25
  286.3 15.5 %copy-start.1 = (f32[128,2048]{1,0:T(8,128)S(1)}, f32[128,2048]{1,0:T(8,128)}, u32[]{:S(2)}) copy-start(f32[128,2048]{1,0:T(8,128)} %copy-done) | copy-start | bytes 3145732
  286.3 15.5 %copy-start.41 = (f32[1,2048]{1,0:T(1,128)S(1)}, f32[1,2048]{1,0:T(1,128)}, u32[]{:S(2)}) copy-start(f32[1,2048]{1,0:T(1,128)} %get-tuple-element.285) | copy-start | bytes 24580
  307.4 24.3 %copy-start.23 = (f32[128,8]{1,0:T(8,128)S(1)}, f32[128,8]{1,0:T(8,128)}, u32[]{:S(2)}) copy-start(f32[128,8]{1,0:T(8,128)} %reduce_sum.192) | copy-start | bytes 12292
  308.4 26.2 %copy-start.16 = (f32[2,128,8,128]{3,2,1,0:T(8,128)S(1)}, f32[2,128,8,128]{3,2,1,0:T(8,128)}, u32[]{:S(2)}) copy-start(f32[2,128,8,128]{3,2,1,0:T(8,128)} %get-tuple-element.115) | copy-start | bytes 3145732
  329.3 6.9 %copy-start.10 = (bf16[128,2048]{1,0:T(8,128)(2,1)S(1)}, bf16[128,2048]{1,0:T(8,128)(2,1)}, u32[]{:S(2)}) copy-start(bf16[128,2048]{1,0:T(8,128)(2,1)} %get-tuple-element.241) | copy-start | bytes 1572868
  329.3 7.0 %copy-start.11 = (bf16[128,2048]{1,0:T(8,128)(2,1)S(1)}, bf16[128,2048]{1,0:T(8,128)(2,1)}, u32[]{:S(2)}) copy-start(bf16[128,2048]{1,0:T(8,128)(2,1)} %get-tuple-element.239) | copy-start | bytes 1572868
  334.9 5.0 %collective-permute-start.10 = (bf16[3,2048]{1,0:T(4,128)(2,1)S(1)}, bf16[3,2048]{1,0:T(4,128)(2,1)S(1)}, u32[]{:S(2)}, u32[]{:S(2)}) collective-permute-start(bf16[3,2048]{1,0:T(4,128)(2,1)S(1)} %slice.918), channel_id=1, source_target_pairs={{1,0},{2,1},{3,2},{4,3},{5,4},{6,5},{7,6},{9,8},{10,9},{11,10},{12... | collective-permute-start | bytes 36872 | tf_op jit(solution)/shard_map/ppermute | solution.py:25
  (37 other events, 166.8 us)
Sparse Core Ops, SparseCore 0:
  93.8 31.9 all-gather.7
  153.3 22.3 all-gather.11
  244.5 23.2 all-gather.9
  274.1 38.7 reduce-scatter.1

commit v3 on v2

--- a/solution.py
+++ b/solution.py
@@ -38,48 +38,84 @@
     return sigmoid_v * (1.0 + value * (1.0 - sigmoid_v))
 
 
-def attention_group(group_index, query_heads, grad_heads, key_whole, first_row, softmax_scale):
-    query_g = lax.dynamic_index_in_dim(query_heads, group_index, 1, False)
-    grad_g = lax.dynamic_index_in_dim(grad_heads, group_index, 1, False)
-    pair_rows = lax.dynamic_index_in_dim(key_whole, group_index, 2, False)
-    key_rows = pair_rows[:, 0]
-    value_rows = pair_rows[:, 1]
-    scores = (
-        jnp.einsum("trd,sd->trs", query_g, key_rows, preferred_element_type=jnp.float32)
-        * softmax_scale
-    )
-    query_pos = first_row + jnp.arange(query_g.shape[0], dtype=jnp.int32)
-    key_pos = jnp.arange(key_rows.shape[0], dtype=jnp.int32)
-    allowed = (key_pos[None, :] <= query_pos[:, None])[:, None, :]
-    row_peak = jnp.max(jnp.where(allowed, scores, -jnp.inf), axis=-1, keepdims=True)
-    row_total = jnp.sum(jnp.where(allowed, jnp.exp(scores - row_peak), 0.0), axis=-1, keepdims=True)
-    probs_b = jnp.where(allowed, jnp.exp(scores - (row_peak + jnp.log(row_total))), 0.0).astype(
-        jnp.bfloat16
-    )
-    output = jnp.einsum(
-        "trs,sd->trd", probs_b, value_rows, preferred_element_type=jnp.float32
-    ).astype(jnp.bfloat16)
-    prob_slope = jnp.einsum("trd,sd->trs", grad_g, value_rows, preferred_element_type=jnp.float32)
-    row_delta = jnp.sum(
-        grad_g.astype(jnp.float32) * output.astype(jnp.float32), axis=-1, keepdims=True
-    )
-    score_grad = (probs_b.astype(jnp.float32) * (prob_slope - row_delta)).astype(jnp.bfloat16)
-    query_grad = (
-        jnp.einsum("trs,sd->trd", score_grad, key_rows, preferred_element_type=jnp.float32)
-        * softmax_scale
-    ).astype(jnp.bfloat16)
-    return (output, query_grad, probs_b, score_grad)
-
-
-def key_terms(probs_all, score_all, query_heads, grad_heads, softmax_scale):
-    key_grad = (
-        jnp.einsum("gtrs,tgrd->sgd", score_all, query_heads, preferred_element_type=jnp.float32)
-        * softmax_scale
-    )
-    value_grad = jnp.einsum(
-        "gtrs,tgrd->sgd", probs_all, grad_heads, preferred_element_type=jnp.float32
-    )
-    return jnp.stack([key_grad, value_grad], axis=1)
+def attention_kernel(row_ref, q_ref, kv_ref, g_ref, o_ref, dq_ref, dkv_ref):
+    rows = q_ref.shape[0]
+    seq = kv_ref.shape[0]
+    width = HDIM
+    groups = kv_ref.shape[1] // (2 * width)
+    heads = q_ref.shape[1] // width // groups
+    scale = width ** (-0.5)
+    query_pos = row_ref[0] + lax.broadcasted_iota(jnp.int32, (rows, seq), 0)
+    key_pos = lax.broadcasted_iota(jnp.int32, (rows, seq), 1)
+    allowed = key_pos <= query_pos
+
+    def group(g, carry):
+        key_col = pl.multiple_of(g * width, width)
+        value_col = pl.multiple_of((groups + g) * width, width)
+        keys = kv_ref[:, pl.ds(key_col, width)]
+        values = kv_ref[:, pl.ds(value_col, width)]
+        key_acc = jnp.zeros((seq, width), jnp.float32)
+        value_acc = jnp.zeros((seq, width), jnp.float32)
+        for r in range(heads):
+            col = pl.multiple_of((g * heads + r) * width, width)
+            cols = pl.ds(col, width)
+            query = q_ref[:, cols]
+            grad = g_ref[:, cols]
+            scores = lax.dot_general(
+                query, keys, (((1,), (1,)), ((), ())), preferred_element_type=jnp.float32
+            ) * scale
+            masked = jnp.where(allowed, scores, -jnp.inf)
+            peak = jnp.max(masked, axis=-1, keepdims=True)
+            total = jnp.sum(jnp.exp(masked - peak), axis=-1, keepdims=True)
+            probs = jnp.exp(masked - (peak + jnp.log(total))).astype(jnp.bfloat16)
+            output = jnp.dot(probs, values, preferred_element_type=jnp.float32).astype(
+                jnp.bfloat16
+            )
+            o_ref[:, cols] = output
+            slope = lax.dot_general(
+                grad, values, (((1,), (1,)), ((), ())), preferred_element_type=jnp.float32
+            )
+            delta = jnp.sum(
+                grad.astype(jnp.float32) * output.astype(jnp.float32), axis=-1, keepdims=True
+            )
+            score_grad = (probs.astype(jnp.float32) * (slope - delta)).astype(jnp.bfloat16)
+            dq_ref[:, cols] = (
+                jnp.dot(score_grad, keys, preferred_element_type=jnp.float32) * scale
+            ).astype(jnp.bfloat16)
+            key_acc = key_acc + lax.dot_general(
+                score_grad, query, (((0,), (0,)), ((), ())), preferred_element_type=jnp.float32
+            )
+            value_acc = value_acc + lax.dot_general(
+                probs, grad, (((0,), (0,)), ((), ())), preferred_element_type=jnp.float32
+            )
+        dkv_ref[:, pl.ds(key_col, width)] = (key_acc * scale).astype(jnp.bfloat16)
+        dkv_ref[:, pl.ds(value_col, width)] = value_acc.astype(jnp.bfloat16)
+        return carry
+
+    lax.fori_loop(0, groups, group, 0)
+
+
+def attention(first_row, query_in, pairs_whole, attn_grad):
+    rows = query_in.shape[0]
+    seq = pairs_whole.shape[0]
+    smem = pl.BlockSpec(memory_space=pltpu.SMEM)
+    whole = pl.BlockSpec(memory_space=pltpu.VMEM)
+    flops = 12 * rows * seq * query_in.shape[1]
+    return pl.pallas_call(
+        attention_kernel,
+        in_specs=[smem, whole, whole, whole],
+        out_specs=[whole, whole, whole],
+        out_shape=[
+            jax.ShapeDtypeStruct(query_in.shape, jnp.bfloat16),
+            jax.ShapeDtypeStruct(query_in.shape, jnp.bfloat16),
+            jax.ShapeDtypeStruct(pairs_whole.shape, jnp.bfloat16),
+        ],
+        cost_estimate=pl.CostEstimate(
+            flops=flops,
+            transcendentals=2 * rows * seq * query_in.shape[1] // HDIM,
+            bytes_accessed=2 * (4 * query_in.size + 2 * pairs_whole.size),
+        ),
+    )(first_row.reshape(1), query_in, pairs_whole, attn_grad)
 
 
 LANES = 128
@@ -258,6 +294,33 @@
 
 def flat_view(stacked):
     return stacked.reshape(stacked.shape[0], stacked.shape[1] * stacked.shape[2])
+
+
+def ctx_scan(decay_sum, carried, rates, axis, backward):
+    count = lax.axis_size(axis)
+    step = -1 if backward else 1
+    merged = passed_along(jnp.concatenate([decay_sum, carried], axis=0), axis, step)
+    distance = 1
+    while distance < count:
+        other = passed_along(merged, axis, step * distance)
+        own_sum = merged[:1]
+        merged = jnp.concatenate(
+            [own_sum + other[:1], jnp.exp(rates * own_sum) * other[1:] + merged[1:]], axis=0
+        )
+        distance *= 2
+    return merged[1:]
+
+
+def ctx_total(parts, axis):
+    count = lax.axis_size(axis)
+    if count & (count - 1):
+        return jnp.sum(lax.all_gather(parts, axis), axis=0)
+    distance = 1
+    while distance < count:
+        pairs = [(i, i ^ distance) for i in range(count)]
+        parts = parts + lax.ppermute(parts, axis, pairs)
+        distance *= 2
+    return parts
 
 
 def mamba_chunk(mixture, mamba_grad, proj_in, conv_taps, conv_shift, log_rates, direct_gain):
@@ -288,25 +351,9 @@
     gy_r = lanes_view(out_drive)
     a_r = lanes_view(decay_rate)
     state_end, adjoint_end = mamba_summary(b_flat, c_flat, dt_r, u_r, gy_r, a_r)
-    step_total = jnp.sum(dt_r, axis=0)
-    gathered = lax.all_gather(
-        jnp.concatenate([state_end, adjoint_end, step_total[None]], axis=0), "ctx"
-    )
-    count = a_r.shape[0]
-    place = lax.axis_index("ctx")
-    devices = gathered.shape[0]
-    state_in = jnp.zeros_like(state_end)
-    adjoint_in = jnp.zeros_like(adjoint_end)
-    for other in range(devices):
-        decay = jnp.exp(a_r * gathered[other, 2 * count][None])
-        state_in = jnp.where(
-            other < place, decay * state_in + gathered[other, :count], state_in
-        )
-    for other in reversed(range(devices)):
-        decay = jnp.exp(a_r * gathered[other, 2 * count][None])
-        adjoint_in = jnp.where(
-            other > place, decay * adjoint_in + gathered[other, count : 2 * count], adjoint_in
-        )
+    step_total = jnp.sum(dt_r, axis=0, keepdims=True)
+    state_in = ctx_scan(step_total, state_end, a_r, "ctx", False)
+    adjoint_in = ctx_scan(step_total, adjoint_end, a_r, "ctx", True)
     y_ssm, moved_grad, step_ssm, rate_grad_r, c_fold, b_fold = mamba_full(
         b_flat, c_flat, dt_r, u_r, gy_r, a_r, state_in, adjoint_in
     )
@@ -336,7 +383,7 @@
     log_grad = rate_grad * decay_rate
     weight_parts = jnp.concatenate(
         [tap_grad, bias_grad[None], log_grad, skip_grad[None]], axis=0
-    ).astype(jnp.bfloat16)
+    )
     mix_out = jnp.stack([signal_grad, gating_grad, raw_grad]).astype(jnp.bfloat16)
     return mamba_out, mix_out, b_grad, c_grad, weight_parts
 
@@ -359,7 +406,7 @@
         (mix_in[0], mamba_cot[0], query_in, pair_in, attn_grad)
     )
     channels = mix_local.shape[-1]
-    pieces = 2 if channels % (2 * ROWS * LANES) == 0 else 1
+    pieces = 1
     width = channels // pieces
     arrived = []
     for piece in range(pieces):
@@ -371,34 +418,17 @@
             )
         arrived.append((shifted(mix_part, "section", 1), shifted(cot_part, "section", -1)))
     row_count = query_in.shape[0]
-    group_size = HEADS // KVHEADS
-    softmax_scale = HDIM ** (-0.5)
-    first_row = lax.axis_index("ctx") * row_count
+    first_row = (lax.axis_index("ctx") * row_count).astype(jnp.int32)
     pairs_whole = lax.all_gather(pair_in, "ctx", axis=0, tiled=True)
     seq_length = pairs_whole.shape[0]
-    key_whole = pairs_whole.reshape(seq_length, 2, KVHEADS, HDIM)
-    query_heads = query_in.reshape(row_count, KVHEADS, group_size, HDIM)
-    grad_heads = attn_grad.reshape(row_count, KVHEADS, group_size, HDIM)
-
-    def per_group(group_index):
-        return attention_group(
-            group_index, query_heads, grad_heads, key_whole, first_row, softmax_scale
-        )
-
-    outputs, query_grads, probs_all, score_all = lax.map(
-        per_group, jnp.arange(KVHEADS, dtype=jnp.int32)
-    )
-    attn_out = outputs.transpose(1, 0, 2, 3).reshape(row_count, HEADS * HDIM)
-    query_out = query_grads.transpose(1, 0, 2, 3).reshape(row_count, HEADS * HDIM)
-    whole_term = key_terms(probs_all, score_all, query_heads, grad_heads, softmax_scale)
+    attn_out, query_out, pair_grad = attention(first_row, query_in, pairs_whole, attn_grad)
+    whole_term = pair_grad
     first_mix, first_cot, attn_out, query_out, whole_term = lax.optimization_barrier(
         arrived[0] + (attn_out, query_out, whole_term)
     )
     arrived[0] = (first_mix, first_cot)
-    key_sum = lax.psum_scatter(
-        whole_term.astype(jnp.bfloat16), "ctx", scatter_dimension=0, tiled=True
-    )
-    pair_out = key_sum.reshape(row_count, 2 * KVHEADS * HDIM)
+    key_sum = lax.psum_scatter(whole_term, "ctx", scatter_dimension=0, tiled=True)
+    pair_out = key_sum
     results = []
     for piece, (mix_part, cot_part) in enumerate(arrived):
         cut = slice(piece * width, (piece + 1) * width)
@@ -418,7 +448,7 @@
     b_grad = sum(r[2] for r in results)
     c_grad = sum(r[3] for r in results)
     weight_parts = jnp.concatenate([r[4] for r in results], axis=1)
-    weight_sum = jnp.sum(lax.all_gather(weight_parts, "ctx").astype(jnp.float32), axis=0)
+    weight_sum = ctx_total(weight_parts, "ctx")
     taps = conv_weight.shape[1]
     states = a_log.shape[1]
     tap_sum = weight_sum[:taps]

time: 353 us -> 310 us (0.88)
  waiting for transfers between devices: 105 us -> 148 us
  other arithmetic: 66.2 us -> 32.9 us
  matrix products: 31.3 us -> 0 us
  local copies, waits for them, and re-layouts: 45.3 us -> 14.4 us
  starting transfers between devices: 17 us -> 42.7 us
  blocking collectives: 19.9 us -> 0 us
  Pallas kernels: 43.4 us -> 56.8 us
  loops' own time: 7.91 us -> 0 us
    dot_general x18 -> x0, matrix products: 31.3 us -> none  [the longest x4 9.67 us: attention_group(): jnp.einsum('trd,sd->trs', grad_g, value_rows, preferred_element_type=jnp....]
    ppermute x0 -> x3, waiting for transfers between devices: none -> 27.6 us  [ctx_total(): parts = parts + lax.ppermute(parts, axis, pairs)]
    ppermute x4 -> x10, waiting for transfers between devices: 0.01 us -> 24.2 us  [passed_along(): return lax.ppermute(shard, axis, pairs)]
    all_gather x1 -> x0, blocking collectives: 19.9 us -> none  [body(): lax.all_gather(weight_parts, 'ctx').astype(jnp.float32)]
    ppermute x4 -> x10, starting transfers between devices: 5.15 us -> 24.8 us  [passed_along(): return lax.ppermute(shard, axis, pairs)]
    pallas_call x0 -> x1, Pallas kernels: none -> 18.2 us  [attention(): pl.pallas_call(attention_kernel, in_specs=[smem, whole, whole, whole], ou...]
    ppermute x8 -> x6, waiting for transfers between devices: 105 us -> 95.9 us  [shifted(): return lax.ppermute(block, axis, route)]
    reduce_sum x11 -> x1, other arithmetic: 9.55 us -> 1.25 us  [mamba_chunk(): step_total = jnp.sum(dt_r, axis=0, keepdims=True)]
  transfers between devices with their start and end apart: 16 -> 21, of which waited for: 4 -> 12; matrix products, arithmetic and copies ran while one was open for 38% -> 6% of each run, Pallas kernels for 12% -> 6%
where the time goes in v3:
time: 310 us; the launch traced here: 309 us
  waiting for transfers between devices  148 us (48%)
  Pallas kernels  56.8 us (18%)
  starting transfers between devices  42.7 us (14%)
  other arithmetic  32.9 us (11%)
  between operations  14.5 us (5%)
  local copies, waits for them, and re-layouts  14.4 us (5%)
    ppermute x6, waiting for transfers between devices, shifted(): return lax.ppermute(block, axis, route)  95.9 us
    pallas_call x1, Pallas kernels, mamba_full(): pl.pallas_call(full_kernel, grid=(blocks,), in_specs=[smem, smem, rows, r...  28 us
    ppermute x3, waiting for transfers between devices, ctx_total(): parts = parts + lax.ppermute(parts, axis, pairs)  27.6 us
    ppermute x10, starting transfers between devices, passed_along(): return lax.ppermute(shard, axis, pairs)  24.8 us
    ppermute x10, waiting for transfers between devices, passed_along(): return lax.ppermute(shard, axis, pairs)  24.2 us
    pallas_call x1, Pallas kernels, attention(): pl.pallas_call(attention_kernel, in_specs=[smem, whole, whole, whole], ou...  18.2 us
    pallas_call x1, Pallas kernels, mamba_summary(): pl.pallas_call(summary_kernel, grid=(blocks,), in_specs=[smem, smem, rows...  10.5 us
    reduce_sum x1, other arithmetic, mamba_chunk(): jnp.sum(pre_grad * padded[offset:offset + row_count], axis=0)  10.4 us
  transfers between devices with their start and end apart: 21, of which 12 were waited for; matrix products, arithmetic and copies ran while one was open for 6% of the time, Pallas kernels for 6%

profile of v3, /device:TPU:0, one launch (start us, length us, event | category | flops | bytes accessed | tf_op | source)
XLA Modules:
  0.0 309.0 jit_solution(6559313260666913768)
XLA Ops:
  7.2 3.0 collective-permute-start.1
  10.2 7.5 %collective-permute-done.1 = bf16[128,1024]{1,0:T(8,128)(2,1)S(1)} collective-permute-done((bf16[128,1024]{1,0:T(8,128)(2,1)}, bf16[128,1024]{1,0:T(8,128)(2,1)S(1)}, u32[]{:S(2)}, u32[]{:S(2)}) %collective-permute-start.1) | collective-permute-done | bytes 262176 | tf_op jit(solution)/shard_map/ppermute | solution.py:19
  19.3 2.2 collective-permute-start.2
  21.5 13.0 %collective-permute-done.q_ref = bf16[128,2048]{1,0:T(8,128)(2,1)S(1)} collective-permute-done((bf16[128,2048]{1,0:T(8,128)(2,1)}, bf16[128,2048]{1,0:T(8,128)(2,1)S(1)}, u32[]{:S(2)}, u32[]{:S(2)}) %collective-permute-start) | collective-permute-done | bytes 524320 | tf_op jit(solution)/shard_map/ppermute | solution.py:19
  34.5 9.4 %collective-permute-done.2.g_ref = bf16[128,2048]{1,0:T(8,128)(2,1)S(1)} collective-permute-done((bf16[128,2048]{1,0:T(8,128)(2,1)}, bf16[128,2048]{1,0:T(8,128)(2,1)S(1)}, u32[]{:S(2)}, u32[]{:S(2)}) %collective-permute-start.2) | collective-permute-done | bytes 524320 | tf_op jit(solution)/shard_map/ppermute | solution.py:19
  50.1 66.0 %collective-permute-done.5 = bf16[128,16]{0,1:T(8,128)(2,1)S(1)} collective-permute-done((bf16[128,16]{0,1:T(8,128)(2,1)}, bf16[128,16]{0,1:T(8,128)(2,1)S(1)}, u32[]{:S(2)}, u32[]{:S(2)}) %collective-permute-start.5) | collective-permute-done | bytes 4128 | tf_op jit(solution)/shard_map/ppermute | solution.py:19
  117.7 18.2 %shard_map.177 = (bf16[128,2048]{1,0:T(8,128)(2,1)}, bf16[128,2048]{1,0:T(8,128)(2,1)}, bf16[1024,1024]{1,0:T(8,128)(2,1)}) custom-call(s32[1]{0:T(128)} %bitcast.5.row_ref, bf16[128,2048]{1,0:T(8,128)(2,1)} %copy-done.15, bf16[1024,1024]{1,0:T(8,128)(2,1)} %all-gather.2.cloned.1.call-done.kv_ref, bf16[128,2048]{1,0:T(8,128)(2,1)} %copy-done.16), custom_call_target="tpu_custom_call" | custom-call | flops 3221225472 | bytes 6291456 | tf_op jit(solution)/shard_map/pallas_call | solution.py:104
  138.0 2.4 compare_select_fusion.2.dt_ref
  143.5 3.7 %multiply_reduce_fusion = (f32[4096]{0:T(1024)}, f32[128,4096]{1,0:T(8,128)S(1)}, f32[16,8,32,128]{3,1,2,0:T(8,128)S(1)}) fusion(bf16[128,4096]{1,0:T(8,128)(2,1)} %collective-permute-done.4, bf16[3,128,4096]{2,1,0:T(8,128)(2,1)S(1)} %copy-done.2, f32[131,4096]{1,0:T(8,128)S(1)} %maximum_convert_fusion, f32[4096]{0:T(1024)S(1)} %bitcast.199, ...), kind=kLoop, calls=%fused_computation.62 | loop fusion | flops 11005952 | bytes 14778368 | tf_op jit(solution)/shard_map/reduce_sum | solution.py:366
  147.3 2.0 copy.31
  149.3 1.6 multiply_bitcast_fusion
  150.9 1.7 copy.30
  152.6 10.5 %shard_map.178 = (f32[8,32,128]{2,1,0:T(8,128)}, f32[8,32,128]{2,1,0:T(8,128)}) custom-call(f32[1024]{0:T(1024)} %reshape.168.b_ref, f32[1024]{0:T(1024)} %reshape.170.c_ref, f32[128,32,128]{2,1,0:T(8,128)} %compare_select_fusion.2.dt_ref, f32[128,32,128]{2,1,0:T(8,128)} %bitcast.191, f32[128,32,128]{2,1,0:T(8,128)} %bitcast.189, f32[8,32,128]{2,1,0:T(8,128)} %bitcast.208), custom_call_target="tpu_custom_call" | custom-call | flops 37748736 | bytes 6291456 | tf_op jit(solution)/shard_map/pallas_call | solution.py:250
  165.4 3.8 %collective-permute-done.11 = f32[9,32,128]{2,1,0:T(8,128)S(1)} collective-permute-done((f32[9,32,128]{2,1,0:T(8,128)S(1)}, f32[9,32,128]{2,1,0:T(8,128)S(1)}, u32[]{:S(2)}, u32[]{:S(2)}) %collective-permute-start.11) | collective-permute-done | bytes 147488 | tf_op jit(solution)/shard_map/ppermute | solution.py:25
  170.4 6.2 %collective-permute-start.7 = (f32[9,32,128]{2,1,0:T(8,128)S(1)}, f32[9,32,128]{2,1,0:T(8,128)S(1)}, u32[]{:S(2)}, u32[]{:S(2)}) collective-permute-start(f32[9,32,128]{2,1,0:T(8,128)S(1)} %get-tuple-element.85), channel_id=1, source_target_pairs={{0,1},{1,2},{2,3},{3,4},{4,5},{5,6},{6,7},{8,9},{9,10},{10,11},{11... | collective-permute-start | bytes 442376 | tf_op jit(solution)/shard_map/ppermute | solution.py:25
  178.3 4.5 %collective-permute-start.8 = (f32[9,32,128]{2,1,0:T(8,128)S(1)}, f32[9,32,128]{2,1,0:T(8,128)S(1)}, u32[]{:S(2)}, u32[]{:S(2)}) collective-permute-start(f32[9,32,128]{2,1,0:T(8,128)S(1)} %collective-permute-done.7), channel_id=1, source_target_pairs={{0,1},{1,2},{2,3},{3,4},{4,5},{5,6},{6,7},{8,9},{9,10},{10,11},{11... | collective-permute-start | bytes 442376 | tf_op jit(solution)/shard_map/ppermute | solution.py:25
  182.8 1.8 collective-permute-done.13
  186.0 11.1 %collective-permute-done.14 = f32[9,32,128]{2,1,0:T(8,128)S(1)} collective-permute-done((f32[9,32,128]{2,1,0:T(8,128)S(1)}, f32[9,32,128]{2,1,0:T(8,128)S(1)}, u32[]{:S(2)}, u32[]{:S(2)}) %collective-permute-start.14) | collective-permute-done | bytes 147488 | tf_op jit(solution)/shard_map/ppermute | solution.py:25
  197.8 1.6 collective-permute-start.9
  199.4 3.3 %collective-permute-done.9 = f32[9,32,128]{2,1,0:T(8,128)S(1)} collective-permute-done((f32[9,32,128]{2,1,0:T(8,128)S(1)}, f32[9,32,128]{2,1,0:T(8,128)S(1)}, u32[]{:S(2)}, u32[]{:S(2)}) %collective-permute-start.9) | collective-permute-done | bytes 147488 | tf_op jit(solution)/shard_map/ppermute | solution.py:25
  202.8 4.5 %collective-permute-start.10 = (f32[9,32,128]{2,1,0:T(8,128)S(1)}, f32[9,32,128]{2,1,0:T(8,128)S(1)}, u32[]{:S(2)}, u32[]{:S(2)}) collective-permute-start(f32[9,32,128]{2,1,0:T(8,128)S(1)} %pad_maximum_fusion.5), channel_id=1, source_target_pairs={{0,4},{1,5},{2,6},{3,7},{8,12},{9,13},{10,14},{11,15},{16,20},{17,... | collective-permute-start | bytes 442376 | tf_op jit(solution)/shard_map/ppermute | solution.py:25
  207.4 2.9 collective-permute-done.10
  210.9 28.0 %shard_map.179 = (f32[128,32,128]{2,1,0:T(8,128)}, f32[128,32,128]{2,1,0:T(8,128)}, f32[128,32,128]{2,1,0:T(8,128)}, f32[8,32,128]{2,1,0:T(8,128)}, f32[4,128,8,...) custom-call(f32[1024]{0:T(1024)} %reshape.168.b_ref, f32[1024]{0:T(1024)} %reshape.170.c_ref, ...), custom_call_target="tpu_custom_call" | custom-call | flops 125829120 | bytes 12582912 | tf_op jit(solution)/shard_map/pallas_call | solution.py:271
  240.0 10.4 %multiply_reduce_fusion.1 = (f32[4096]{0:T(1024)}, f32[4096]{0:T(1024)}, f32[4096]{0:T(1024)}, f32[4096]{0:T(1024)}, f32[4096]{0:T(1024)}, /*index=5*/f32[128,40...) fusion(f32[131,4096]{1,0:T(8,128)S(1)} %maximum_convert_fusion, ...), kind=kLoop, calls=%fused_computation.63 | loop fusion | flops 27766784 | bytes 25264128 | tf_op jit(solution)/shard_map/reduce_sum | solution.py:380
  250.4 2.0 concatenate.61
  253.1 1.9 reduce_sum.82
  255.0 1.8 reduce_sum.83
  261.4 4.4 %collective-permute-start.17 = (f32[14,4096]{1,0:T(8,128)S(1)}, f32[14,4096]{1,0:T(8,128)S(1)}, u32[]{:S(2)}, u32[]{:S(2)}) collective-permute-start(f32[14,4096]{1,0:T(8,128)S(1)} %add.136), channel_id=1, source_target_pairs={{0,2},{1,3},{2,0},{3,1},{4,6},{5,7},{6,4},{7,5},{8,10},{9,11},{10,... | collective-permute-start | bytes 688136 | tf_op jit(solution)/shard_map/ppermute | solution.py:321
  266.8 11.3 %collective-permute-done.17 = f32[14,4096]{1,0:T(8,128)S(1)} collective-permute-done((f32[14,4096]{1,0:T(8,128)S(1)}, f32[14,4096]{1,0:T(8,128)S(1)}, u32[]{:S(2)}, u32[]{:S(2)}) %collective-permute-start.17) | collective-permute-done | bytes 229408 | tf_op jit(solution)/shard_map/ppermute | solution.py:321
  278.2 3.7 %collective-permute-start.18 = (f32[14,4096]{1,0:T(8,128)S(1)}, f32[14,4096]{1,0:T(8,128)S(1)}, u32[]{:S(2)}, u32[]{:S(2)}) collective-permute-start(f32[14,4096]{1,0:T(8,128)S(1)} %add.137), channel_id=1, source_target_pairs={{0,4},{1,5},{2,6},{3,7},{4,0},{5,1},{6,2},{7,3},{8,12},{9,13},{10,... | collective-permute-start | bytes 688136 | tf_op jit(solution)/shard_map/ppermute | solution.py:321
  281.9 2.0 pad_maximum_fusion
  283.9 16.3 %collective-permute-done.18 = f32[14,4096]{1,0:T(8,128)S(1)} collective-permute-done((f32[14,4096]{1,0:T(8,128)S(1)}, f32[14,4096]{1,0:T(8,128)S(1)}, u32[]{:S(2)}, u32[]{:S(2)}) %collective-permute-start.18) | collective-permute-done | bytes 229408 | tf_op jit(solution)/shard_map/ppermute | solution.py:321
  (99 shorter events, 31.8 us)
Async XLA Ops:
  7.2 110.5 %all-gather.2.cloned.1.call-start = ((), (), s32[]{:S(2)}) async-start(), calls=%async_computation.1 | async-start | bytes 2359296 | tf_op jit(solution)/shard_map/all_gather | solution.py:422
  7.2 10.5 %collective-permute-start.1 = (bf16[128,1024]{1,0:T(8,128)(2,1)}, bf16[128,1024]{1,0:T(8,128)(2,1)S(1)}, u32[]{:S(2)}, u32[]{:S(2)}) collective-permute-start(bf16[128,1024]{1,0:T(8,128)(2,1)} %bitcast.223), channel_id=1, source_target_pairs={{24,0},{0,8},{8,16},{16,24},{25,1},{1,9},{9,17},{17,25},{26,2},{2,... | collective-permute-start | bytes 786440 | tf_op jit(solution)/shard_map/ppermute | solution.py:19
  18.4 283.7 %reduce-scatter.2.cloned.1.call-start = ((), (), s32[]{:S(2)}) async-start(), calls=%async_computation.2 | async-start | bytes 2359296 | tf_op jit(solution)/shard_map/reduce_scatter | solution.py:430
  18.5 16.0 %collective-permute-start = (bf16[128,2048]{1,0:T(8,128)(2,1)}, bf16[128,2048]{1,0:T(8,128)(2,1)S(1)}, u32[]{:S(2)}, u32[]{:S(2)}) collective-permute-start(bf16[128,2048]{1,0:T(8,128)(2,1)} %bitcast.221), channel_id=1, source_target_pairs={{24,0},{0,8},{8,16},{16,24},{25,1},{1,9},{9,17},{17,25},{26,2},{2,... | collective-permute-start | bytes 1572872 | tf_op jit(solution)/shard_map/ppermute | solution.py:19
  19.3 24.6 %collective-permute-start.2 = (bf16[128,2048]{1,0:T(8,128)(2,1)}, bf16[128,2048]{1,0:T(8,128)(2,1)S(1)}, u32[]{:S(2)}, u32[]{:S(2)}) collective-permute-start(bf16[128,2048]{1,0:T(8,128)(2,1)} %bitcast.222), channel_id=1, source_target_pairs={{8,0},{16,8},{24,16},{0,24},{9,1},{17,9},{25,17},{1,25},{10,2},{18... | collective-permute-start | bytes 1572872 | tf_op jit(solution)/shard_map/ppermute | solution.py:19
  34.5 11.5 %copy-start.15 = (bf16[128,2048]{1,0:T(8,128)(2,1)}, bf16[128,2048]{1,0:T(8,128)(2,1)S(1)}, u32[]{:S(2)}) copy-start(bf16[128,2048]{1,0:T(8,128)(2,1)S(1)} %collective-permute-done.q_ref) | copy-start | bytes 1572868
  43.9 92.1 %collective-permute-start.3 = (bf16[3,128,4096]{2,1,0:T(8,128)(2,1)}, bf16[3,128,4096]{2,1,0:T(8,128)(2,1)S(1)}, u32[]{:S(2)}, u32[]{:S(2)}) collective-permute-start(bf16[3,128,4096]{2,1,0:T(8,128)(2,1)} %bitcast.219), channel_id=1, source_target_pairs={{24,0},{0,8},{8,16},{16,24},{25,1},{1,9},{9,17},{17,25},{26,2},{2,... | collective-permute-start | bytes 9437192 | tf_op jit(solution)/shard_map/ppermute | solution.py:19
  44.5 71.6 %collective-permute-start.5 = (bf16[128,16]{0,1:T(8,128)(2,1)}, bf16[128,16]{0,1:T(8,128)(2,1)S(1)}, u32[]{:S(2)}, u32[]{:S(2)}) collective-permute-start(bf16[128,16]{0,1:T(8,128)(2,1)} %bitcast.225), channel_id=1, source_target_pairs={{24,0},{0,8},{8,16},{16,24},{25,1},{1,9},{9,17},{17,25},{26,2},{2,... | collective-permute-start | bytes 12296 | tf_op jit(solution)/shard_map/ppermute | solution.py:19
  46.0 90.0 %collective-permute-start.4 = (bf16[128,4096]{1,0:T(8,128)(2,1)}, bf16[128,4096]{1,0:T(8,128)(2,1)}, u32[]{:S(2)}, u32[]{:S(2)}) collective-permute-start(bf16[128,4096]{1,0:T(8,128)(2,1)} %bitcast.220), channel_id=1, source_target_pairs={{8,0},{16,8},{24,16},{0,24},{9,1},{17,9},{25,17},{1,25},{10,2},{18... | collective-permute-start | bytes 3145736 | tf_op jit(solution)/shard_map/ppermute | solution.py:19
  48.5 93.5 %copy-start.8 = (f32[1,1,4096]{2,1,0:T(1,128)}, f32[1,1,4096]{2,1,0:T(1,128)S(1)}, u32[]{:S(2)}) copy-start(f32[1,1,4096]{2,1,0:T(1,128)S(1)} %get-tuple-element.81) | copy-start | bytes 49156
  48.5 93.5 %copy-start.10 = (f32[1,1,4096]{2,1,0:T(1,128)}, f32[1,1,4096]{2,1,0:T(1,128)S(1)}, u32[]{:S(2)}) copy-start(f32[1,1,4096]{2,1,0:T(1,128)S(1)} %get-tuple-element.82) | copy-start | bytes 49156
  48.5 93.5 %copy-start.12 = (f32[1,1,4096]{2,1,0:T(1,128)}, f32[1,1,4096]{2,1,0:T(1,128)S(1)}, u32[]{:S(2)}) copy-start(f32[1,1,4096]{2,1,0:T(1,128)S(1)} %get-tuple-element.83) | copy-start | bytes 49156
  136.0 4.4 %copy-start.1 = (bf16[3,128,4096]{2,1,0:T(8,128)(2,1)}, bf16[3,128,4096]{2,1,0:T(8,128)(2,1)S(1)}, u32[]{:S(2)}) copy-start(bf16[3,128,4096]{2,1,0:T(8,128)(2,1)S(1)} %collective-permute-done.3) | copy-start | bytes 9437188
  136.3 5.4 %collective-permute-start.6 = (bf16[3,4096]{1,0:T(4,128)(2,1)S(1)}, bf16[3,4096]{1,0:T(4,128)(2,1)S(1)}, u32[]{:S(2)}, u32[]{:S(2)}) collective-permute-start(bf16[3,4096]{1,0:T(4,128)(2,1)S(1)} %slice_bitcast_fusion.3), channel_id=1, source_target_pairs={{0,1},{1,2},{2,3},{3,4},{4,5},{5,6},{6,7},{8,9},{9,10},{10,11},{11... | collective-permute-start | bytes 73736 | tf_op jit(solution)/shard_map/ppermute | solution.py:25
  164.1 5.1 %collective-permute-start.11 = (f32[9,32,128]{2,1,0:T(8,128)S(1)}, f32[9,32,128]{2,1,0:T(8,128)S(1)}, u32[]{:S(2)}, u32[]{:S(2)}) collective-permute-start(f32[9,32,128]{2,1,0:T(8,128)S(1)} %get-tuple-element.84), channel_id=1, source_target_pairs={{1,0},{2,1},{3,2},{4,3},{5,4},{6,5},{7,6},{9,8},{10,9},{11,10},{12... | collective-permute-start | bytes 442376 | tf_op jit(solution)/shard_map/ppermute | solution.py:25
  169.2 7.5 %collective-permute-start.12 = (f32[9,32,128]{2,1,0:T(8,128)S(1)}, f32[9,32,128]{2,1,0:T(8,128)S(1)}, u32[]{:S(2)}, u32[]{:S(2)}) collective-permute-start(f32[9,32,128]{2,1,0:T(8,128)S(1)} %collective-permute-done.11), channel_id=1, source_target_pairs={{1,0},{2,1},{3,2},{4,3},{5,4},{6,5},{7,6},{9,8},{10,9},{11,10},{12... | collective-permute-start | bytes 442376 | tf_op jit(solution)/shard_map/ppermute | solution.py:25
  170.4 7.8 %collective-permute-start.7 = (f32[9,32,128]{2,1,0:T(8,128)S(1)}, f32[9,32,128]{2,1,0:T(8,128)S(1)}, u32[]{:S(2)}, u32[]{:S(2)}) collective-permute-start(f32[9,32,128]{2,1,0:T(8,128)S(1)} %get-tuple-element.85), channel_id=1, source_target_pairs={{0,1},{1,2},{2,3},{3,4},{4,5},{5,6},{6,7},{8,9},{9,10},{10,11},{11... | collective-permute-start | bytes 442376 | tf_op jit(solution)/shard_map/ppermute | solution.py:25
  176.8 7.8 %collective-permute-start.13 = (f32[9,32,128]{2,1,0:T(8,128)S(1)}, f32[9,32,128]{2,1,0:T(8,128)S(1)}, u32[]{:S(2)}, u32[]{:S(2)}) collective-permute-start(f32[9,32,128]{2,1,0:T(8,128)S(1)} %pad_maximum_fusion.6), channel_id=1, source_target_pairs={{2,0},{3,1},{4,2},{5,3},{6,4},{7,5},{10,8},{11,9},{12,10},{13,11},... | collective-permute-start | bytes 442376 | tf_op jit(solution)/shard_map/ppermute | solution.py:25
  178.3 7.7 %collective-permute-start.8 = (f32[9,32,128]{2,1,0:T(8,128)S(1)}, f32[9,32,128]{2,1,0:T(8,128)S(1)}, u32[]{:S(2)}, u32[]{:S(2)}) collective-permute-start(f32[9,32,128]{2,1,0:T(8,128)S(1)} %collective-permute-done.7), channel_id=1, source_target_pairs={{0,1},{1,2},{2,3},{3,4},{4,5},{5,6},{6,7},{8,9},{9,10},{10,11},{11... | collective-permute-start | bytes 442376 | tf_op jit(solution)/shard_map/ppermute | solution.py:25
  184.6 12.4 %collective-permute-start.14 = (f32[9,32,128]{2,1,0:T(8,128)S(1)}, f32[9,32,128]{2,1,0:T(8,128)S(1)}, u32[]{:S(2)}, u32[]{:S(2)}) collective-permute-start(f32[9,32,128]{2,1,0:T(8,128)S(1)} %pad_maximum_fusion.7), channel_id=1, source_target_pairs={{4,0},{5,1},{6,2},{7,3},{12,8},{13,9},{14,10},{15,11},{20,16},{21,... | collective-permute-start | bytes 442376 | tf_op jit(solution)/shard_map/ppermute | solution.py:25
  197.8 4.9 %collective-permute-start.9 = (f32[9,32,128]{2,1,0:T(8,128)S(1)}, f32[9,32,128]{2,1,0:T(8,128)S(1)}, u32[]{:S(2)}, u32[]{:S(2)}) collective-permute-start(f32[9,32,128]{2,1,0:T(8,128)S(1)} %pad_maximum_fusion.4), channel_id=1, source_target_pairs={{0,2},{1,3},{2,4},{3,5},{4,6},{5,7},{8,10},{9,11},{10,12},{11,13},... | collective-permute-start | bytes 442376 | tf_op jit(solution)/shard_map/ppermute | solution.py:25
  202.8 7.4 %collective-permute-start.10 = (f32[9,32,128]{2,1,0:T(8,128)S(1)}, f32[9,32,128]{2,1,0:T(8,128)S(1)}, u32[]{:S(2)}, u32[]{:S(2)}) collective-permute-start(f32[9,32,128]{2,1,0:T(8,128)S(1)} %pad_maximum_fusion.5), channel_id=1, source_target_pairs={{0,4},{1,5},{2,6},{3,7},{8,12},{9,13},{10,14},{11,15},{16,20},{17,... | collective-permute-start | bytes 442376 | tf_op jit(solution)/shard_map/ppermute | solution.py:25
  210.9 28.0 %copy-start.6 = (f32[1,8,4096]{2,1,0:T(8,128)S(1)}, f32[1,8,4096]{2,1,0:T(8,128)}, u32[]{:S(2)}) copy-start(f32[1,8,4096]{2,1,0:T(8,128)} %param.18) | copy-start | bytes 393220
  252.4 2.6 copy-start.5
  252.4 7.9 %collective-permute-start.16 = (f32[14,4096]{1,0:T(8,128)S(1)}, f32[14,4096]{1,0:T(8,128)}, u32[]{:S(2)}, u32[]{:S(2)}) collective-permute-start(f32[14,4096]{1,0:T(8,128)S(1)} %concatenate.61), channel_id=1, source_target_pairs={{0,1},{1,0},{2,3},{3,2},{4,5},{5,4},{6,7},{7,6},{8,9},{9,8},{10,11... | collective-permute-start | bytes 688136 | tf_op jit(solution)/shard_map/ppermute | solution.py:321
  253.1 12.7 %copy-start.9 = (f32[1,1,4096]{2,1,0:T(1,128)S(1)}, f32[1,1,4096]{2,1,0:T(1,128)}, u32[]{:S(2)}) copy-start(f32[1,1,4096]{2,1,0:T(1,128)} %copy-done.8) | copy-start | bytes 49156
  253.1 12.7 %copy-start.11 = (f32[1,1,4096]{2,1,0:T(1,128)S(1)}, f32[1,1,4096]{2,1,0:T(1,128)}, u32[]{:S(2)}) copy-start(f32[1,1,4096]{2,1,0:T(1,128)} %copy-done.10) | copy-start | bytes 49156
  253.1 12.7 %copy-start.13 = (f32[1,1,4096]{2,1,0:T(1,128)S(1)}, f32[1,1,4096]{2,1,0:T(1,128)}, u32[]{:S(2)}) copy-start(f32[1,1,4096]{2,1,0:T(1,128)} %copy-done.12) | copy-start | bytes 49156
  256.9 3.3 %collective-permute-start.15 = (bf16[3,4096]{1,0:T(4,128)(2,1)}, bf16[3,4096]{1,0:T(4,128)(2,1)S(1)}, u32[]{:S(2)}, u32[]{:S(2)}) collective-permute-start(bf16[3,4096]{1,0:T(4,128)(2,1)} %slice.283), channel_id=1, source_target_pairs={{1,0},{2,1},{3,2},{4,3},{5,4},{6,5},{7,6},{9,8},{10,9},{11,10},{12... | collective-permute-start | bytes 73736 | tf_op jit(solution)/shard_map/ppermute | solution.py:25
  261.4 20.5 %copy-start.4 = (bf16[1,1,128,4096]{3,2,1,0:T(8,128)(2,1)S(1)}, bf16[1,1,128,4096]{3,2,1,0:T(8,128)(2,1)}, u32[]{:S(2)}) copy-start(bf16[1,1,128,4096]{3,2,1,0:T(8,128)(2,1)} %get-tuple-element.68) | copy-start | bytes 3145732
  261.4 16.7 %collective-permute-start.17 = (f32[14,4096]{1,0:T(8,128)S(1)}, f32[14,4096]{1,0:T(8,128)S(1)}, u32[]{:S(2)}, u32[]{:S(2)}) collective-permute-start(f32[14,4096]{1,0:T(8,128)S(1)} %add.136), channel_id=1, source_target_pairs={{0,2},{1,3},{2,0},{3,1},{4,6},{5,7},{6,4},{7,5},{8,10},{9,11},{10,... | collective-permute-start | bytes 688136 | tf_op jit(solution)/shard_map/ppermute | solution.py:321
  278.2 22.0 %collective-permute-start.18 = (f32[14,4096]{1,0:T(8,128)S(1)}, f32[14,4096]{1,0:T(8,128)S(1)}, u32[]{:S(2)}, u32[]{:S(2)}) collective-permute-start(f32[14,4096]{1,0:T(8,128)S(1)} %add.137), channel_id=1, source_target_pairs={{0,4},{1,5},{2,6},{3,7},{4,0},{5,1},{6,2},{7,3},{8,12},{9,13},{10,... | collective-permute-start | bytes 688136 | tf_op jit(solution)/shard_map/ppermute | solution.py:321
  (6 other events, 10.7 us)
Sparse Core Ops, SparseCore 0:
  18.5 29.6 all-gather.1
  252.6 45.1 reduce-scatter.1

commit v4 on v3

--- a/solution.py
+++ b/solution.py
@@ -296,21 +296,6 @@
     return stacked.reshape(stacked.shape[0], stacked.shape[1] * stacked.shape[2])
 
 
-def ctx_scan(decay_sum, carried, rates, axis, backward):
-    count = lax.axis_size(axis)
-    step = -1 if backward else 1
-    merged = passed_along(jnp.concatenate([decay_sum, carried], axis=0), axis, step)
-    distance = 1
-    while distance < count:
-        other = passed_along(merged, axis, step * distance)
-        own_sum = merged[:1]
-        merged = jnp.concatenate(
-            [own_sum + other[:1], jnp.exp(rates * own_sum) * other[1:] + merged[1:]], axis=0
-        )
-        distance *= 2
-    return merged[1:]
-
-
 def ctx_total(parts, axis):
     count = lax.axis_size(axis)
     if count & (count - 1):
@@ -323,7 +308,7 @@
     return parts
 
 
-def mamba_chunk(mixture, mamba_grad, proj_in, conv_taps, conv_shift, log_rates, direct_gain):
+def mamba_chunk(mixture, mamba_grad, proj_in, conv_taps, conv_shift, log_rates, direct_gain, fence):
     signal = mixture[0]
     gating = mixture[1]
     unscaled_step = mixture[2]
@@ -351,11 +336,33 @@
     gy_r = lanes_view(out_drive)
     a_r = lanes_view(decay_rate)
     state_end, adjoint_end = mamba_summary(b_flat, c_flat, dt_r, u_r, gy_r, a_r)
-    step_total = jnp.sum(dt_r, axis=0, keepdims=True)
-    state_in = ctx_scan(step_total, state_end, a_r, "ctx", False)
-    adjoint_in = ctx_scan(step_total, adjoint_end, a_r, "ctx", True)
+    step_total = jnp.sum(dt_r, axis=0)
+    own_decay = jnp.exp(a_r * step_total[None])
+    gathered = lax.all_gather(
+        jnp.concatenate([state_end, adjoint_end, own_decay], axis=0).astype(jnp.bfloat16), "ctx"
+    ).astype(jnp.float32)
+    gathered, fence = lax.optimization_barrier((gathered, fence))
+    fence = lax.psum_scatter(fence, "ctx", scatter_dimension=0, tiled=True)
+    count = a_r.shape[0]
+    place = lax.axis_index("ctx")
+    devices = gathered.shape[0]
+    state_in = jnp.zeros_like(state_end)
+    adjoint_in = jnp.zeros_like(adjoint_end)
+    for other in range(devices):
+        decay = gathered[other, 2 * count :]
+        state_in = jnp.where(
+            other < place, decay * state_in + gathered[other, :count], state_in
+        )
+    for other in reversed(range(devices)):
+        decay = gathered[other, 2 * count :]
+        adjoint_in = jnp.where(
+            other > place, decay * adjoint_in + gathered[other, count : 2 * count], adjoint_in
+        )
     y_ssm, moved_grad, step_ssm, rate_grad_r, c_fold, b_fold = mamba_full(
         b_flat, c_flat, dt_r, u_r, gy_r, a_r, state_in, adjoint_in
+    )
+    y_ssm, moved_grad, step_ssm, fence = lax.optimization_barrier(
+        (y_ssm, moved_grad, step_ssm, fence)
     )
     mixed_out = flat_view(y_ssm) + direct_gain * inner_act
     step_grad = flat_view(step_ssm) + flat_view(moved_grad) * inner_act
@@ -385,7 +392,7 @@
         [tap_grad, bias_grad[None], log_grad, skip_grad[None]], axis=0
     )
     mix_out = jnp.stack([signal_grad, gating_grad, raw_grad]).astype(jnp.bfloat16)
-    return mamba_out, mix_out, b_grad, c_grad, weight_parts
+    return mamba_out, mix_out, b_grad, c_grad, weight_parts, fence
 
 
 def body(
@@ -427,8 +434,7 @@
         arrived[0] + (attn_out, query_out, whole_term)
     )
     arrived[0] = (first_mix, first_cot)
-    key_sum = lax.psum_scatter(whole_term, "ctx", scatter_dimension=0, tiled=True)
-    pair_out = key_sum
+    pair_out = whole_term
     results = []
     for piece, (mix_part, cot_part) in enumerate(arrived):
         cut = slice(piece * width, (piece + 1) * width)
@@ -441,14 +447,18 @@
                 conv_bias[0][cut],
                 a_log[0][:, cut],
                 skip_gain[0][cut],
+                pair_out,
             )
         )
+        pair_out = results[-1][5]
     mamba_out = jnp.concatenate([r[0] for r in results], axis=1)
     mix_out = jnp.concatenate([r[1] for r in results], axis=2)
     b_grad = sum(r[2] for r in results)
     c_grad = sum(r[3] for r in results)
     weight_parts = jnp.concatenate([r[4] for r in results], axis=1)
-    weight_sum = ctx_total(weight_parts, "ctx")
+    spare = max(0, 17 - weight_parts.shape[0])
+    padded_parts = jnp.pad(weight_parts, ((0, spare), (0, 0))).astype(jnp.bfloat16)
+    weight_sum = jnp.sum(lax.all_gather(padded_parts, "ctx").astype(jnp.float32), axis=0)
     taps = conv_weight.shape[1]
     states = a_log.shape[1]
     tap_sum = weight_sum[:taps]

time: 310 us -> 274 us (0.88)
  starting transfers between devices: 42.7 us -> 12.5 us
  waiting for transfers between devices: 148 us -> 137 us
  other arithmetic: 32.9 us -> 39.9 us
    all_gather x0 -> x2, waiting for transfers between devices: none -> 38.7 us  [the longest x1 25.3 us: mamba_chunk(): lax.all_gather(jnp.concatenate([state_end, adjoint_end, own_decay], axis=...]
    ppermute x3 -> x0, waiting for transfers between devices: 27.6 us -> none  [ctx_total(): parts = parts + lax.ppermute(parts, axis, pairs)]
    ppermute x10 -> x2, waiting for transfers between devices: 24.2 us -> 1.25 us  [passed_along(): return lax.ppermute(shard, axis, pairs)]
    ppermute x10 -> x2, starting transfers between devices: 24.8 us -> 2.7 us  [passed_along(): return lax.ppermute(shard, axis, pairs)]
    ppermute x3 -> x0, starting transfers between devices: 8.26 us -> none  [ctx_total(): parts = parts + lax.ppermute(parts, axis, pairs)]
    select_n x0 -> x2, other arithmetic: none -> 4.96 us  [the longest x1 2.48 us: mamba_chunk(): jnp.where(other > place, decay * adjoint_in + gathered[other, count:2 * c...]
    convert_element_type x0 -> x1, other arithmetic: none -> 3.51 us  [mamba_chunk(): gathered = lax.all_gather(jnp.concatenate([state_end, adjoint_end, own_de...]
    unnamed x38 -> x27, local copies, waits for them, and re-layouts: 7.04 us -> 7.75 us
  transfers between devices with their start and end apart: 21 -> 12, of which waited for: 12 -> 8; matrix products, arithmetic and copies ran while one was open for 6% -> 8% of each run, Pallas kernels for 6% -> 17%
where the time goes in v4:
time: 274 us
  waiting for transfers between devices  137 us (50%)
  Pallas kernels  56.9 us (21%)
  other arithmetic  39.9 us (15%)
  between operations  14 us (5%)
  local copies, waits for them, and re-layouts  12.9 us (5%)
  starting transfers between devices  12.5 us (5%)
    ppermute x6, waiting for transfers between devices, shifted(): return lax.ppermute(block, axis, route)  96 us
    pallas_call x1, Pallas kernels, mamba_full(): pl.pallas_call(full_kernel, grid=(blocks,), in_specs=[smem, smem, rows, r...  28.1 us
    all_gather x1, waiting for transfers between devices, mamba_chunk(): lax.all_gather(jnp.concatenate([state_end, adjoint_end, own_decay], axis=...  25.3 us
    pallas_call x1, Pallas kernels, attention(): pl.pallas_call(attention_kernel, in_specs=[smem, whole, whole, whole], ou...  18.3 us
    all_gather x1, waiting for transfers between devices, body(): lax.all_gather(padded_parts, 'ctx').astype(jnp.float32)  13.4 us
    pallas_call x1, Pallas kernels, mamba_summary(): pl.pallas_call(summary_kernel, grid=(blocks,), in_specs=[smem, smem, rows...  10.5 us
    reduce_sum x1, other arithmetic, mamba_chunk(): jnp.sum(pre_grad * padded[offset:offset + row_count], axis=0)  9.81 us
    ppermute x6, starting transfers between devices, shifted(): return lax.ppermute(block, axis, route)  9.5 us
  transfers between devices with their start and end apart: 12, of which 8 were waited for; matrix products, arithmetic and copies ran while one was open for 8% of the time, Pallas kernels for 17%

profile of v4, /device:TPU:0, one launch (start us, length us, event | category | flops | bytes accessed | tf_op | source)
XLA Modules:
  0.0 273.8 jit_solution(15711780372001645567)
XLA Ops:
  7.2 3.0 %collective-permute-start.1 = (bf16[128,1024]{1,0:T(8,128)(2,1)}, bf16[128,1024]{1,0:T(8,128)(2,1)S(1)}, u32[]{:S(2)}, u32[]{:S(2)}) collective-permute-start(bf16[128,1024]{1,0:T(8,128)(2,1)} %bitcast.445), channel_id=1, source_target_pairs={{24,0},{0,8},{8,16},{16,24},{25,1},{1,9},{9,17},{17,25},{26,2},{2,... | collective-permute-start | bytes 786440 | tf_op jit(solution)/shard_map/ppermute | solution.py:19
  10.2 7.5 %collective-permute-done.1 = bf16[128,1024]{1,0:T(8,128)(2,1)S(1)} collective-permute-done((bf16[128,1024]{1,0:T(8,128)(2,1)}, bf16[128,1024]{1,0:T(8,128)(2,1)S(1)}, u32[]{:S(2)}, u32[]{:S(2)}) %collective-permute-start.1) | collective-permute-done | bytes 262176 | tf_op jit(solution)/shard_map/ppermute | solution.py:19
  19.3 2.2 collective-permute-start.2
  21.5 13.0 %collective-permute-done.q_ref = bf16[128,2048]{1,0:T(8,128)(2,1)S(1)} collective-permute-done((bf16[128,2048]{1,0:T(8,128)(2,1)}, bf16[128,2048]{1,0:T(8,128)(2,1)S(1)}, u32[]{:S(2)}, u32[]{:S(2)}) %collective-permute-start) | collective-permute-done | bytes 524320 | tf_op jit(solution)/shard_map/ppermute | solution.py:19
  34.5 9.4 %collective-permute-done.2.g_ref = bf16[128,2048]{1,0:T(8,128)(2,1)S(1)} collective-permute-done((bf16[128,2048]{1,0:T(8,128)(2,1)}, bf16[128,2048]{1,0:T(8,128)(2,1)S(1)}, u32[]{:S(2)}, u32[]{:S(2)}) %collective-permute-start.2) | collective-permute-done | bytes 524320 | tf_op jit(solution)/shard_map/ppermute | solution.py:19
  44.5 1.5 collective-permute-start.5
  46.0 1.4 collective-permute-start.4
  50.1 66.0 %collective-permute-done.5 = bf16[128,16]{0,1:T(8,128)(2,1)S(1)} collective-permute-done((bf16[128,16]{0,1:T(8,128)(2,1)}, bf16[128,16]{0,1:T(8,128)(2,1)S(1)}, u32[]{:S(2)}, u32[]{:S(2)}) %collective-permute-start.5) | collective-permute-done | bytes 4128 | tf_op jit(solution)/shard_map/ppermute | solution.py:19
  117.7 18.3 %shard_map.177 = (bf16[128,2048]{1,0:T(8,128)(2,1)}, bf16[128,2048]{1,0:T(8,128)(2,1)}, bf16[1024,1024]{1,0:T(8,128)(2,1)}) custom-call(s32[1]{0:T(128)} %bitcast.5.row_ref, bf16[128,2048]{1,0:T(8,128)(2,1)} %copy-done.9, bf16[1024,1024]{1,0:T(8,128)(2,1)} %all-gather.6.cloned.1.call-done.kv_ref, bf16[128,2048]{1,0:T(8,128)(2,1)} %copy-done.10), custom_call_target="tpu_custom_call" | custom-call | flops 3221225472 | bytes 6291456 | tf_op jit(solution)/shard_map/pallas_call | solution.py:104
  136.0 1.2 fusion.30
  137.6 1.3 collective-permute-start.6
  139.3 2.4 compare_select_fusion.2.dt_ref
  142.1 1.5 copy-done.2
  143.6 3.1 %multiply_reduce_fusion = (bf16[4096]{0:T(1024)(128)(2,1)S(1)}, f32[128,4096]{1,0:T(8,128)S(1)}, f32[16,8,32,128]{3,1,2,0:T(8,128)S(1)}) fusion(bf16[128,4096]{1,0:T(8,128)(2,1)} %collective-permute-done.4, bf16[3,128,4096]{2,1,0:T(8,128)(2,1)S(1)} %copy-done.2, f32[131,4096]{1,0:T(8,128)S(1)} %maximum_convert_fusion, f32[4096]{0:T(1024)S(1)} %bitcast.429, ...), kind=kLoop, calls=%fused_computation.63 | loop fusion | flops 11005952 | bytes 14770176 | tf_op jit(solution)/shard_map/reduce_sum | solution.py:373
  146.8 2.0 copy.31
  148.8 1.6 multiply_bitcast_fusion
  150.3 1.7 copy.30
  152.0 10.5 %shard_map.178 = (f32[8,32,128]{2,1,0:T(8,128)}, f32[8,32,128]{2,1,0:T(8,128)}) custom-call(f32[1024]{0:T(1024)} %reshape.214.b_ref, f32[1024]{0:T(1024)} %reshape.216.c_ref, f32[128,32,128]{2,1,0:T(8,128)} %compare_select_fusion.2.dt_ref, f32[128,32,128]{2,1,0:T(8,128)} %bitcast.423, f32[128,32,128]{2,1,0:T(8,128)} %bitcast.421, f32[8,32,128]{2,1,0:T(8,128)} %bitcast.435), custom_call_target="tpu_custom_call" | custom-call | flops 37748736 | bytes 6291456 | tf_op jit(solution)/shard_map/pallas_call | solution.py:250
  164.5 25.3 %all-gather.8.cloned.1.call-done = bf16[8,24,32,128]{3,2,1,0:T(8,128)(2,1)} async-done(((bf16[1,24,32,128]{3,2,1,0:T(8,128)(2,1)}), bf16[8,24,32,128]{3,2,1,0:T(8,128)(2,1)}) %all-gather.8.cloned.1.call-update) | async-done | bytes 1572880 | tf_op jit(solution)/shard_map/all_gather | solution.py:341
  189.8 3.5 %convert_element_type.79 = f32[8,24,32,128]{3,2,1,0:T(8,128)} convert(bf16[8,24,32,128]{3,2,1,0:T(8,128)(2,1)} %all-gather.8.cloned.1.call-done) | non-fusion elementwise | flops 786432 | bytes 4718592 | tf_op jit(solution)/shard_map/convert_element_type | solution.py:343
  193.4 2.5 fusion.54.hin_ref
  195.9 2.5 fusion.46.gin_ref
  198.4 28.1 %shard_map.179 = (f32[128,32,128]{2,1,0:T(8,128)}, f32[128,32,128]{2,1,0:T(8,128)}, f32[128,32,128]{2,1,0:T(8,128)}, f32[8,32,128]{2,1,0:T(8,128)}, f32[4,128,8,...) custom-call(f32[1024]{0:T(1024)} %reshape.214.b_ref, f32[1024]{0:T(1024)} %reshape.216.c_ref, ...), custom_call_target="tpu_custom_call" | custom-call | flops 125829120 | bytes 12582912 | tf_op jit(solution)/shard_map/pallas_call | solution.py:271
  227.5 1.4 reduce-scatter.2.cloned.1.call-done
  228.9 9.8 %multiply_reduce_fusion.1 = (bf16[4096]{0:T(1024)(128)(2,1)S(1)}, bf16[4096]{0:T(1024)(128)(2,1)S(1)}, bf16[4096]{0:T(1024)(128)(2,1)S(1)}, bf16[4096]{0:T(1024)...) fusion(f32[131,4096]{1,0:T(8,128)S(1)} %maximum_convert_fusion,, ...), kind=kLoop, calls=%fused_computation.64 | loop fusion | flops 27766784 | bytes 25223168 | tf_op jit(solution)/shard_map/reduce_sum | solution.py:387
  239.9 2.0 reduce_sum.91
  241.9 1.8 reduce_sum.92
  243.9 1.4 collective-permute-start.7
  245.9 1.2 collective-permute-done.7
  248.2 2.0 pad_maximum_fusion
  250.2 13.4 %all-gather.10.cloned.1.call-done = bf16[8,17,4096]{2,1,0:T(8,128)(2,1)} async-done(((bf16[1,17,4096]{2,1,0:T(8,128)(2,1)}), bf16[8,17,4096]{2,1,0:T(8,128)(2,1)}) %all-gather.10.cloned.1.call-update) | async-done | bytes 1114128 | tf_op jit(solution)/shard_map/all_gather | solution.py:461
  263.6 1.7 convert_reduce_fusion
  (68 shorter events, 15.4 us)
Async XLA Ops:
  7.2 110.5 %all-gather.6.cloned.1.call-start = ((), (), s32[]{:S(2)}) async-start(), calls=%async_computation.1 | async-start | bytes 2359296 | tf_op jit(solution)/shard_map/all_gather | solution.py:429
  7.2 10.5 %collective-permute-start.1 = (bf16[128,1024]{1,0:T(8,128)(2,1)}, bf16[128,1024]{1,0:T(8,128)(2,1)S(1)}, u32[]{:S(2)}, u32[]{:S(2)}) collective-permute-start(bf16[128,1024]{1,0:T(8,128)(2,1)} %bitcast.445), channel_id=1, source_target_pairs={{24,0},{0,8},{8,16},{16,24},{25,1},{1,9},{9,17},{17,25},{26,2},{2,... | collective-permute-start | bytes 786440 | tf_op jit(solution)/shard_map/ppermute | solution.py:19
  17.7 0.7 copy-start.6
  18.4 171.4 %all-gather.8.cloned.1.call-start = ((), (), s32[]{:S(2)}) async-start(), calls=%async_computation.2 | async-start | bytes 1769472 | tf_op jit(solution)/shard_map/all_gather | solution.py:341
  18.5 16.0 %collective-permute-start = (bf16[128,2048]{1,0:T(8,128)(2,1)}, bf16[128,2048]{1,0:T(8,128)(2,1)S(1)}, u32[]{:S(2)}, u32[]{:S(2)}) collective-permute-start(bf16[128,2048]{1,0:T(8,128)(2,1)} %bitcast.443), channel_id=1, source_target_pairs={{24,0},{0,8},{8,16},{16,24},{25,1},{1,9},{9,17},{17,25},{26,2},{2,... | collective-permute-start | bytes 1572872 | tf_op jit(solution)/shard_map/ppermute | solution.py:19
  19.3 24.6 %collective-permute-start.2 = (bf16[128,2048]{1,0:T(8,128)(2,1)}, bf16[128,2048]{1,0:T(8,128)(2,1)S(1)}, u32[]{:S(2)}, u32[]{:S(2)}) collective-permute-start(bf16[128,2048]{1,0:T(8,128)(2,1)} %bitcast.444), channel_id=1, source_target_pairs={{8,0},{16,8},{24,16},{0,24},{9,1},{17,9},{25,17},{1,25},{10,2},{18... | collective-permute-start | bytes 1572872 | tf_op jit(solution)/shard_map/ppermute | solution.py:19
  34.5 11.5 %copy-start.9 = (bf16[128,2048]{1,0:T(8,128)(2,1)}, bf16[128,2048]{1,0:T(8,128)(2,1)S(1)}, u32[]{:S(2)}) copy-start(bf16[128,2048]{1,0:T(8,128)(2,1)S(1)} %collective-permute-done.q_ref) | copy-start | bytes 1572868
  43.9 2.1 copy-start.10
  43.9 92.1 %collective-permute-start.3 = (bf16[3,128,4096]{2,1,0:T(8,128)(2,1)}, bf16[3,128,4096]{2,1,0:T(8,128)(2,1)S(1)}, u32[]{:S(2)}, u32[]{:S(2)}) collective-permute-start(bf16[3,128,4096]{2,1,0:T(8,128)(2,1)} %bitcast.441), channel_id=1, source_target_pairs={{24,0},{0,8},{8,16},{16,24},{25,1},{1,9},{9,17},{17,25},{26,2},{2,... | collective-permute-start | bytes 9437192 | tf_op jit(solution)/shard_map/ppermute | solution.py:19
  44.5 71.6 %collective-permute-start.5 = (bf16[128,16]{0,1:T(8,128)(2,1)}, bf16[128,16]{0,1:T(8,128)(2,1)S(1)}, u32[]{:S(2)}, u32[]{:S(2)}) collective-permute-start(bf16[128,16]{0,1:T(8,128)(2,1)} %bitcast.447), channel_id=1, source_target_pairs={{24,0},{0,8},{8,16},{16,24},{25,1},{1,9},{9,17},{17,25},{26,2},{2,... | collective-permute-start | bytes 12296 | tf_op jit(solution)/shard_map/ppermute | solution.py:19
  46.0 90.0 %collective-permute-start.4 = (bf16[128,4096]{1,0:T(8,128)(2,1)}, bf16[128,4096]{1,0:T(8,128)(2,1)}, u32[]{:S(2)}, u32[]{:S(2)}) collective-permute-start(bf16[128,4096]{1,0:T(8,128)(2,1)} %bitcast.442), channel_id=1, source_target_pairs={{8,0},{16,8},{24,16},{0,24},{9,1},{17,9},{25,17},{1,25},{10,2},{18... | collective-permute-start | bytes 3145736 | tf_op jit(solution)/shard_map/ppermute | solution.py:19
  136.0 1.7 copy-start.1
  137.6 4.1 %collective-permute-start.6 = (bf16[3,4096]{1,0:T(4,128)(2,1)S(1)}, bf16[3,4096]{1,0:T(4,128)(2,1)S(1)}, u32[]{:S(2)}, u32[]{:S(2)}) collective-permute-start(bf16[3,4096]{1,0:T(4,128)(2,1)S(1)} %slice_bitcast_fusion.3), channel_id=1, source_target_pairs={{0,1},{1,2},{2,3},{3,4},{4,5},{5,6},{6,7},{8,9},{9,10},{10,11},{11... | collective-permute-start | bytes 73736 | tf_op jit(solution)/shard_map/ppermute | solution.py:25
  141.7 1.9 copy-start.2
  141.7 1.9 copy-start.8
  146.8 2.0 copy-start
  164.3 64.7 %reduce-scatter.2.cloned.1.call-start = ((), (), s32[]{:S(2)}) async-start(), calls=%async_computation.3 | async-start | bytes 2359296 | tf_op jit(solution)/shard_map/reduce_scatter | solution.py:345
  193.3 70.3 %all-gather.10.cloned.1.call-start = ((), (), s32[]{:S(2)}) async-start(), calls=%async_computation.4 | async-start | bytes 1769472 | tf_op jit(solution)/shard_map/all_gather | solution.py:461
  198.4 28.1 %copy-start.5 = (f32[1,8,4096]{2,1,0:T(8,128)S(1)}, f32[1,8,4096]{2,1,0:T(8,128)}, u32[]{:S(2)}) copy-start(f32[1,8,4096]{2,1,0:T(8,128)} %param.18) | copy-start | bytes 393220
  198.4 30.6 %copy-start.7 = (f32[1,4096]{1,0:T(1,128)S(1)}, f32[1,4096]{1,0:T(1,128)}, u32[]{:S(2)}) copy-start(f32[1,4096]{1,0:T(1,128)} %param.19) | copy-start | bytes 49156
  239.9 3.9 %copy-start.3 = (f32[128,4096]{1,0:T(8,128)S(1)}, f32[128,4096]{1,0:T(8,128)}, u32[]{:S(2)}) copy-start(f32[128,4096]{1,0:T(8,128)} %get-tuple-element.75) | copy-start | bytes 6291460
  243.9 4.3 %copy-start.4 = (bf16[1,1,128,4096]{3,2,1,0:T(8,128)(2,1)S(1)}, bf16[1,1,128,4096]{3,2,1,0:T(8,128)(2,1)}, u32[]{:S(2)}) copy-start(bf16[1,1,128,4096]{3,2,1,0:T(8,128)(2,1)} %get-tuple-element.80) | copy-start | bytes 3145732
  243.9 3.3 %collective-permute-start.7 = (bf16[3,4096]{1,0:T(4,128)(2,1)S(1)}, bf16[3,4096]{1,0:T(4,128)(2,1)S(1)}, u32[]{:S(2)}, u32[]{:S(2)}) collective-permute-start(bf16[3,4096]{1,0:T(4,128)(2,1)S(1)} %slice.321), channel_id=1, source_target_pairs={{1,0},{2,1},{3,2},{4,3},{5,4},{6,5},{7,6},{9,8},{10,9},{11,10},{12... | collective-permute-start | bytes 73736 | tf_op jit(solution)/shard_map/ppermute | solution.py:25
Sparse Core Ops, SparseCore 0:
  18.5 29.6 all-gather.5
  164.4 25.3 all-gather.7
  193.4 35.4 reduce-scatter.1
  240.1 23.5 all-gather.9
